TPU v7x, 32 devices: a whole 2x2x4 slice. The times are simulated.
32 devices in a mesh: parts: 2 (over y), tm: 4 (over x, core), cols: 4 (over z).
Axes of the slice: x: 2, y: 2, z: 4, core: 2. Of those that a mesh axis runs over, the one named last changes fastest.
Arguments:
- noise: float32 [16, 1024, 1024], P(('parts', 'tm'), None, 'cols'), parts along dimension 0, may hold values from -6 to 6
- inv_diag: float32 [16, 1024, 1024], P(('parts', 'tm'), None, 'cols'), parts along dimension 0, may hold values from -2 to 2, as said below
- coupling: float32 [16, 1024, 1024], P(('parts', 'tm'), None, 'cols'), parts along dimension 0, may hold values from -1 to 1, as said below
- order: int32 [1024], replicated, may hold values from 0 to 1023, each once
Outputs:
- sample: float32 [16, 1024, 1024], P(('parts', 'tm'), None, 'cols'), parts along dimension 0
There are 2 independent parts, one for each index of `parts`. A program takes and returns all parts, laid end to end along the dimension named above; an argument that names none is the same for every part. Nothing has to cross between parts.
Inputs may be any that keep to these rules, and one draw needn't show every extreme that they name: `order`: each of 0 to 1023 appears once. `inv_diag`: diagonal entries lie between 0.5 and 2, off-diagonal entries are small in magnitude. `coupling`: diagonal entries lie between 0.5 and 0.97, off-diagonal entries are small in magnitude.
All inputs are finite; a program needn't handle non-finite values.
Results may differ from a plain program's by a relative error of at most 0.00013.
Values sent between devices are 32-bit elements; how exact they have to be, the bound alone decides.
No kernel may reach another device: no remote copies, remote signals or barrier semaphores. Data moves between devices by JAX's collectives and lax.ppermute only.
A program may use at most 128 MiB of HBM per device.

v0:
```python
import jax
import jax.numpy as jnp
from jax import lax
from jax.sharding import PartitionSpec as P

precise = lax.Precision.HIGHEST


def shifted(block, axis, distance):
    devices = range(lax.axis_size(axis))
    route = [(i - distance, i) for i in devices if i - distance in devices]
    return lax.ppermute(block, axis, route)


def fold_with(operand, segment):
    return jnp.dot(segment, operand, precision=precise, preferred_element_type=jnp.float32)


def shards(noise, inv_diag, coupling, order):
    block_count = noise.shape[0]
    sample_count = noise.shape[2]
    driven = jnp.einsum(
        "kmn,kns->kms",
        lax.all_gather(inv_diag, "cols", axis=2, tiled=True),
        noise,
        precision=precise,
        preferred_element_type=jnp.float32,
    )
    local_field = driven[block_count - 1]
    reduced = coupling[block_count - 1]
    block = 0
    operand = jnp.concatenate([local_field, reduced], axis=1)
    product = fold_with(operand, lax.all_gather(coupling[block], "cols", axis=1, tiled=True))
    local_field = driven[block] + product[:, :sample_count]
    reduced = product[:, sample_count:]
    reduced_full = lax.all_gather(reduced, "cols", axis=1, tiled=True)

    def relay_step(step, carry):
        current, incoming = carry
        incoming = shifted(current, "tm", -1)
        current = local_field + jnp.dot(
            reduced_full, incoming, precision=precise, preferred_element_type=jnp.float32
        )
        return (current, incoming)

    _, entering = lax.fori_loop(
        0, lax.axis_size("tm"), relay_step, (local_field, jnp.zeros_like(local_field))
    )
    carried = entering
    results = [None] * block_count
    for block in range(block_count - 1, -1, -1):
        product = fold_with(carried, lax.all_gather(coupling[block], "cols", axis=1, tiled=True))
        carried = driven[block] + product
        results[block] = carried
    stacked = jnp.stack(results, axis=0)
    return jnp.take(stacked, order, axis=1)


def solution(mesh):
    return jax.shard_map(
        shards,
        mesh=mesh,
        in_specs=(
            P(("parts", "tm"), None, "cols"),
            P(("parts", "tm"), None, "cols"),
            P(("parts", "tm"), None, "cols"),
            P(),
        ),
        out_specs=P(("parts", "tm"), None, "cols"),
        check_vma=False,
    )
```

profile of v0, /device:TPU:25, one launch (start us, length us, event | category | flops | bytes accessed | tf_op | source)
XLA Modules:
  0.0 541.9 jit_solution(10568745071062961867)
XLA Ops:
  7.3 3.1 fusion.32
  12.0 144.7 %all-gather.7.cloned.1.call-done = f32[2,1024,1024]{2,1,0:T(8,128)} async-done(((f32[2,1024,256]{2,1,0:T(8,128)}), f32[2,1024,1024]{2,1,0:T(8,128)}) %all-gather.7.cloned.1.call-update) | async-done | bytes 8388624 | tf_op jit(solution)/shard_map/all_gather | solution.py:24
  156.7 9.8 %fusion.33 = f32[2,1024,256]{1,2,0:T(8,128)S(1)} fusion(f32[2,1024,1024]{2,1,0:T(8,128)} %all-gather.7.cloned.1.call-done, f32[2,1024,256]{2,1,0:T(8,128)S(1)} %copy-done), kind=kOutput, calls=%fused_computation.28 | convolution fusion | flops 6442450944 | bytes 12582912 | tf_op jit(solution)/shard_map/kmn,kns->kms/dot_general | solution.py:22
  168.9 68.7 %all-gather.11.cloned.1.call-done = f32[1,1024,1024]{2,1,0:T(8,128)} async-done(((f32[1,1024,256]{2,1,0:T(8,128)}), f32[1,1024,1024]{2,1,0:T(8,128)}) %all-gather.11.cloned.1.call-update) | async-done | bytes 4194320 | tf_op jit(solution)/shard_map/all_gather | solution.py:52
  237.6 9.5 %fusion.9 = f32[1024,512]{0,1:T(8,128)S(1)} fusion(f32[1,1024,1024]{2,1,0:T(8,128)} %all-gather.11.cloned.1.call-done, f32[1024,256]{0,1:T(8,128)S(1)} %bitcast.59, f32[1024,256]{0,1:T(8,128)} %slice_bitcast_fusion), kind=kOutput, calls=%fused_computation.13 | convolution fusion | flops 6442975232 | bytes 8388608 | tf_op jit(solution)/shard_map/dot_general | solution.py:16
  252.0 76.2 %all-gather.9.cloned.1.call-done = f32[1024,1024]{0,1:T(8,128)} async-done(((f32[1024,256]{0,1:T(8,128)}), f32[1024,1024]{0,1:T(8,128)}) %all-gather.9.cloned.1.call-update) | async-done | bytes 4194320 | tf_op jit(solution)/shard_map/all_gather | solution.py:36
  328.2 5.4 %copy.14 = f32[1024,1024]{1,0:T(8,128)} copy(f32[1024,1024]{0,1:T(8,128)} %all-gather.9.cloned.1.call-done) | data formatting | bytes 8388608 | tf_op jit(solution)/shard_map/while | solution.py:46
  333.6 75.3 %all-gather.13.cloned.1.call-done = f32[1,1024,1024]{1,2,0:T(8,128)} async-done(((f32[1,1024,256]{1,2,0:T(8,128)}), f32[1,1024,1024]{1,2,0:T(8,128)}) %all-gather.13.cloned.1.call-update) | async-done | bytes 4194320 | tf_op jit(solution)/shard_map/all_gather | solution.py:52
  408.9 93.3 %while.12 = (s32[]{:T(128)}, f32[1024,256]{1,0:T(8,128)}, f32[1024,256]{1,0:T(8,128)}, f32[1024,1024]{1,0:T(8,128)}, f32[1024,256]{1,0:T(8,128)S(1)}, /*index=5*/s32[]{:T(128)}) while((s32[]{:T(128)}, f32[1024,256]{1,0:T(8,128)}, f32[1024,256]{1,0:T(8,128)}, f32[1024,1024]{1,0:T(8,128)}, f32[1024,256]{1,0:T(8,128)S(1)}, ...), condition=%wide.region_1.0_spmd, body=%wide.region_0.0_spmd.sunk | while | flops 3221487616 | bytes 11534445 | solution.py:46
  408.9 2.4 collective-permute-start
  411.3 14.1 %collective-permute-done = f32[1024,256]{1,0:T(8,128)} collective-permute-done((f32[1024,256]{1,0:T(8,128)}, f32[1024,256]{1,0:T(8,128)}, u32[]{:S(2)}, u32[]{:S(2)}) %collective-permute-start) | collective-permute-done | bytes 1048608 | tf_op jit(solution)/shard_map/while/body/eval_jaxpr/ppermute | solution.py:12
  425.4 6.9 %convolution_add_fusion.2 = f32[1024,256]{1,0:T(8,128)} fusion(f32[1024,256]{1,0:T(8,128)S(1)} %get-tuple-element.101, f32[1024,1024]{1,0:T(8,128)} %get-tuple-element.100, f32[1024,256]{1,0:T(8,128)} %collective-permute-done), kind=kOutput, calls=%fused_computation.1.clone.1 | convolution fusion | flops 3221487616 | bytes 7340032 | tf_op jit(solution)/shard_map/while/body/eval_jaxpr/dot_general | solution.py:41
  432.3 1.9 collective-permute-start
  434.2 14.5 %collective-permute-done = f32[1024,256]{1,0:T(8,128)} collective-permute-done((f32[1024,256]{1,0:T(8,128)}, f32[1024,256]{1,0:T(8,128)}, u32[]{:S(2)}, u32[]{:S(2)}) %collective-permute-start) | collective-permute-done | bytes 1048608 | tf_op jit(solution)/shard_map/while/body/eval_jaxpr/ppermute | solution.py:12
  448.7 6.9 %convolution_add_fusion.2 = f32[1024,256]{1,0:T(8,128)} fusion(f32[1024,256]{1,0:T(8,128)S(1)} %get-tuple-element.101, f32[1024,1024]{1,0:T(8,128)} %get-tuple-element.100, f32[1024,256]{1,0:T(8,128)} %collective-permute-done), kind=kOutput, calls=%fused_computation.1.clone.1 | convolution fusion | flops 3221487616 | bytes 7340032 | tf_op jit(solution)/shard_map/while/body/eval_jaxpr/dot_general | solution.py:41
  457.5 14.5 %collective-permute-done = f32[1024,256]{1,0:T(8,128)} collective-permute-done((f32[1024,256]{1,0:T(8,128)}, f32[1024,256]{1,0:T(8,128)}, u32[]{:S(2)}, u32[]{:S(2)}) %collective-permute-start) | collective-permute-done | bytes 1048608 | tf_op jit(solution)/shard_map/while/body/eval_jaxpr/ppermute | solution.py:12
  472.0 6.9 %convolution_add_fusion.2 = f32[1024,256]{1,0:T(8,128)} fusion(f32[1024,256]{1,0:T(8,128)S(1)} %get-tuple-element.101, f32[1024,1024]{1,0:T(8,128)} %get-tuple-element.100, f32[1024,256]{1,0:T(8,128)} %collective-permute-done), kind=kOutput, calls=%fused_computation.1.clone.1 | convolution fusion | flops 3221487616 | bytes 7340032 | tf_op jit(solution)/shard_map/while/body/eval_jaxpr/dot_general | solution.py:41
  480.8 14.5 %collective-permute-done = f32[1024,256]{1,0:T(8,128)} collective-permute-done((f32[1024,256]{1,0:T(8,128)}, f32[1024,256]{1,0:T(8,128)}, u32[]{:S(2)}, u32[]{:S(2)}) %collective-permute-start) | collective-permute-done | bytes 1048608 | tf_op jit(solution)/shard_map/while/body/eval_jaxpr/ppermute | solution.py:12
  495.3 6.9 %convolution_add_fusion.2 = f32[1024,256]{1,0:T(8,128)} fusion(f32[1024,256]{1,0:T(8,128)S(1)} %get-tuple-element.101, f32[1024,1024]{1,0:T(8,128)} %get-tuple-element.100, f32[1024,256]{1,0:T(8,128)} %collective-permute-done), kind=kOutput, calls=%fused_computation.1.clone.1 | convolution fusion | flops 3221487616 | bytes 7340032 | tf_op jit(solution)/shard_map/while/body/eval_jaxpr/dot_general | solution.py:41
  502.2 6.6 %fusion.26 = f32[1024,256]{0,1:T(8,128)S(1)} fusion(f32[1024,256]{1,0:T(8,128)} %get-tuple-element.31, f32[1,1024,1024]{1,2,0:T(8,128)} %all-gather.13.cloned.1.call-done, f32[2,1024,256]{1,2,0:T(8,128)} %copy-done.1), kind=kOutput, calls=%fused_computation.18 | convolution fusion | flops 3221487616 | bytes 7340032 | tf_op jit(solution)/shard_map/dot_general | solution.py:16
  508.8 3.7 fusion.20
  514.0 4.1 copy.16
  518.2 10.5 %gather_fusion = f32[1024,2,256]{2,1,0:T(2,128)} fusion(f32[2,1024,256]{2,0,1:T(2,128)} %copy.16, s32[1024]{0:T(1024)S(1)} %fusion.29), kind=kCustom, calls=%fused_computation | custom fusion | bytes 4198400 | tf_op jit(solution)/shard_map/jit(_take)/gather | solution.py:56
  528.6 5.2 select_bitcast_fusion
  (34 shorter events, 16.4 us)
Async XLA Ops:
  6.5 150.2 %copy-start = (f32[2,1024,256]{2,1,0:T(8,128)S(1)}, f32[2,1024,256]{2,1,0:T(8,128)}, u32[]{:S(2)}) copy-start(f32[2,1024,256]{2,1,0:T(8,128)} %param.6) | copy-start | bytes 6291460
  6.5 150.2 %all-gather.7.cloned.1.call-start = ((), (), s32[]{:S(2)}) async-start(), calls=%async_computation | async-start | bytes 10485760 | tf_op jit(solution)/shard_map/all_gather | solution.py:24
  7.3 230.4 %all-gather.11.cloned.1.call-start = ((), (), s32[]{:S(2)}) async-start(), calls=%async_computation.2 | async-start | bytes 5242880 | tf_op jit(solution)/shard_map/all_gather | solution.py:52
  10.4 317.8 %all-gather.9.cloned.1.call-start = ((), (), s32[]{:S(2)}) async-start(), calls=%async_computation.1 | async-start | bytes 5242880 | tf_op jit(solution)/shard_map/all_gather | solution.py:36
  12.0 225.6 %copy-start.5 = (f32[1,1024,256]{1,2,0:T(8,128)}, f32[1,1024,256]{1,2,0:T(8,128)S(1)}, u32[]{:S(2)}) copy-start(f32[1,1024,256]{1,2,0:T(8,128)S(1)} %copy.19) | copy-start | bytes 3145732
  166.5 1.3 copy-start.1
  237.6 9.5 %copy-start.2 = (f32[2,1024,256]{1,2,0:T(8,128)S(1)}, f32[2,1024,256]{1,2,0:T(8,128)}, u32[]{:S(2)}) copy-start(f32[2,1024,256]{1,2,0:T(8,128)} %copy-done.1) | copy-start | bytes 6291460
  248.7 0.7 copy-start.6
  248.7 160.2 %all-gather.13.cloned.1.call-start = ((), (), s32[]{:S(2)}) async-start(), calls=%async_computation.3 | async-start | bytes 5242880 | tf_op jit(solution)/shard_map/all_gather | solution.py:52
  408.9 16.5 %collective-permute-start = (f32[1024,256]{1,0:T(8,128)}, f32[1024,256]{1,0:T(8,128)}, u32[]{:S(2)}, u32[]{:S(2)}) collective-permute-start(f32[1024,256]{1,0:T(8,128)} %get-tuple-element.92), channel_id=1, source_target_pairs={{4,0},{8,4},{12,8},{5,1},{9,5},{13,9},{6,2},{10,6},{14,10},{7,3},{... | collective-permute-start | bytes 3145736 | tf_op jit(solution)/shard_map/while/body/eval_jaxpr/ppermute | solution.py:12
  432.3 16.4 %collective-permute-start = (f32[1024,256]{1,0:T(8,128)}, f32[1024,256]{1,0:T(8,128)}, u32[]{:S(2)}, u32[]{:S(2)}) collective-permute-start(f32[1024,256]{1,0:T(8,128)} %get-tuple-element.92), channel_id=1, source_target_pairs={{4,0},{8,4},{12,8},{5,1},{9,5},{13,9},{6,2},{10,6},{14,10},{7,3},{... | collective-permute-start | bytes 3145736 | tf_op jit(solution)/shard_map/while/body/eval_jaxpr/ppermute | solution.py:12
  455.6 16.4 %collective-permute-start = (f32[1024,256]{1,0:T(8,128)}, f32[1024,256]{1,0:T(8,128)}, u32[]{:S(2)}, u32[]{:S(2)}) collective-permute-start(f32[1024,256]{1,0:T(8,128)} %get-tuple-element.92), channel_id=1, source_target_pairs={{4,0},{8,4},{12,8},{5,1},{9,5},{13,9},{6,2},{10,6},{14,10},{7,3},{... | collective-permute-start | bytes 3145736 | tf_op jit(solution)/shard_map/while/body/eval_jaxpr/ppermute | solution.py:12
  478.9 16.4 %collective-permute-start = (f32[1024,256]{1,0:T(8,128)}, f32[1024,256]{1,0:T(8,128)}, u32[]{:S(2)}, u32[]{:S(2)}) collective-permute-start(f32[1024,256]{1,0:T(8,128)} %get-tuple-element.92), channel_id=1, source_target_pairs={{4,0},{8,4},{12,8},{5,1},{9,5},{13,9},{6,2},{10,6},{14,10},{7,3},{... | collective-permute-start | bytes 3145736 | tf_op jit(solution)/shard_map/while/body/eval_jaxpr/ppermute | solution.py:12
  502.2 6.6 %copy-start.3 = (f32[2,1024,256]{1,2,0:T(8,128)S(1)}, f32[2,1024,256]{1,2,0:T(8,128)}, u32[]{:S(2)}) copy-start(f32[2,1024,256]{1,2,0:T(8,128)} %copy-done.1) | copy-start | bytes 6291460
  502.2 6.6 %copy-start.4 = (f32[1,1024,1024]{2,1,0:T(8,128)S(1)}, f32[1,1024,1024]{2,1,0:T(8,128)}, u32[]{:S(2)}) copy-start(f32[1,1024,1024]{2,1,0:T(8,128)} %all-gather.11.cloned.1.call-done) | copy-start | bytes 12582916
Sparse Core Ops, SparseCore 0:
  8.9 147.7 all-gather.6
  158.3 79.2 all-gather.10
  248.8 79.2 all-gather.8
  329.6 79.2 all-gather.12
where the time goes:
time: 546 us; the launch traced here: 542 us
  waiting for transfers between devices  424 us (78%)
  matrix products  57.1 us (10%)
  local copies, waits for them, and re-layouts  31.2 us (6%)
  between operations  13.2 us (2%)
  starting transfers between devices  8.39 us (2%)
  other arithmetic  8.28 us (2%)
    all_gather x1, waiting for transfers between devices, shards(): lax.all_gather(inv_diag, 'cols', axis=2, tiled=True)  145 us
    all_gather x2, waiting for transfers between devices, shards(): lax.all_gather(coupling[block], 'cols', axis=1, tiled=True)  144 us
    all_gather x1, waiting for transfers between devices, shards(): reduced_full = lax.all_gather(reduced, 'cols', axis=1, tiled=True)  76.2 us
    ppermute x4, waiting for transfers between devices, shifted(): return lax.ppermute(block, axis, route)  57.6 us
    dot_general x4, matrix products, relay_step(): jnp.dot(reduced_full, incoming, precision=precise, preferred_element_type...  27.6 us
    dot_general x3, matrix products, fold_with(): jnp.dot(segment, operand, precision=precise, preferred_element_type=jnp.f...  19.8 us
  transfers between devices with their start and end apart: 8, of which 8 were waited for; matrix products, arithmetic and copies ran while one was open for 4% of the time, Pallas kernels for 0%

commit v1 on v0

v1 whole, which is shorter than its diff:
```python
import jax
import jax.numpy as jnp
from jax import lax
from jax.sharding import PartitionSpec as P

precise = lax.Precision.HIGHEST


def shifted(block, axis, distance):
    devices = range(lax.axis_size(axis))
    route = [(i - distance, i) for i in devices if i - distance in devices]
    return lax.ppermute(block, axis, route)


def apply(matrix, operand):
    return jnp.dot(matrix, operand, precision=precise, preferred_element_type=jnp.float32)


def shards(noise, inv_diag, coupling, order):
    block_count = noise.shape[0]
    inv_full = lax.all_gather(inv_diag, "cols", axis=2, tiled=True)
    coupling_full = lax.all_gather(coupling, "cols", axis=2, tiled=True)
    driven = jnp.einsum(
        "kmn,kns->kms", inv_full, noise, precision=precise, preferred_element_type=jnp.float32
    )

    def chain(entering):
        carried = entering
        results = [None] * block_count
        for block in range(block_count - 1, -1, -1):
            carried = driven[block] + apply(coupling_full[block], carried)
            results[block] = carried
        return results

    def relay_step(step, entering):
        return shifted(chain(entering)[0], "tm", -1)

    entering = lax.fori_loop(0, lax.axis_size("tm") - 1, relay_step, jnp.zeros_like(driven[0]))
    stacked = jnp.stack(chain(entering), axis=0)
    return jnp.take(stacked, order, axis=1)


def solution(mesh):
    return jax.shard_map(
        shards,
        mesh=mesh,
        in_specs=(
            P(("parts", "tm"), None, "cols"),
            P(("parts", "tm"), None, "cols"),
            P(("parts", "tm"), None, "cols"),
            P(),
        ),
        out_specs=P(("parts", "tm"), None, "cols"),
        check_vma=False,
    )
```

time: 546 us -> 439 us (0.80)
  waiting for transfers between devices: 424 us -> 329 us
  local copies, waits for them, and re-layouts: 31.2 us -> 18.1 us
    all_gather x4 -> x2, waiting for transfers between devices: 365 us -> 285 us  [the longest x1 149 us: shards(): inv_full = lax.all_gather(inv_diag, 'cols', axis=2, tiled=True)]
    ppermute x4 -> x3, waiting for transfers between devices: 57.6 us -> 42.8 us  [shifted(): return lax.ppermute(block, axis, route)]
    dot_general x8 -> x9, matrix products: 57.1 us -> 61.6 us  [the longest x8 51.6 us: apply(): jnp.dot(matrix, operand, precision=precise, preferred_element_type=jnp.fl...]
  transfers between devices with their start and end apart: 8 -> 5, of which waited for: 8 -> 5; matrix products, arithmetic and copies ran while one was open for 4% -> 3% of each run, Pallas kernels for 0% -> 0%
where the time goes in v1:
time: 439 us; the launch traced here: 434 us
  waiting for transfers between devices  329 us (75%)
  matrix products  61.6 us (14%)
  local copies, waits for them, and re-layouts  18.1 us (4%)
  between operations  13.5 us (3%)
  starting transfers between devices  6.21 us (1%)
  other arithmetic  5.39 us (1%)
    all_gather x1, waiting for transfers between devices, shards(): inv_full = lax.all_gather(inv_diag, 'cols', axis=2, tiled=True)  149 us
    all_gather x1, waiting for transfers between devices, shards(): coupling_full = lax.all_gather(coupling, 'cols', axis=2, tiled=True)  136 us
    dot_general x8, matrix products, apply(): jnp.dot(matrix, operand, precision=precise, preferred_element_type=jnp.fl...  51.6 us
    ppermute x3, waiting for transfers between devices, shifted(): return lax.ppermute(block, axis, route)  42.8 us
    gather x1, local copies, waits for them, and re-layouts, shards(): return jnp.take(stacked, order, axis=1)  10.5 us
    dot_general x1, matrix products, shards(): jnp.einsum('kmn,kns->kms', inv_full, noise, precision=precise, preferred_...  10 us
  transfers between devices with their start and end apart: 5, of which 5 were waited for; matrix products, arithmetic and copies ran while one was open for 3% of the time, Pallas kernels for 0%

profile of v1, /device:TPU:25, one launch (start us, length us, event | category | flops | bytes accessed | tf_op | source)
XLA Modules:
  0.0 434.1 jit_solution(10742862378299724351)
XLA Ops:
  6.5 0.7 all-gather.3.cloned.1.call-update
  8.0 148.7 %all-gather.3.cloned.1.call-done = f32[2,1024,1024]{2,1,0:T(8,128)} async-done(((f32[2,1024,256]{2,1,0:T(8,128)}), f32[2,1024,1024]{2,1,0:T(8,128)}) %all-gather.3.cloned.1.call-update) | async-done | bytes 8388624 | tf_op jit(solution)/shard_map/all_gather | solution.py:21
  156.7 10.0 %fusion.23 = f32[2,1024,256]{2,1,0:T(8,128)} fusion(f32[2,1024,1024]{2,1,0:T(8,128)} %all-gather.3.cloned.1.call-done, f32[2,1024,256]{2,1,0:T(8,128)S(1)} %copy-done), kind=kOutput, calls=%fused_computation.26 | convolution fusion | flops 6442450944 | bytes 12582912 | tf_op jit(solution)/shard_map/kmn,kns->kms/dot_general | solution.py:23
  166.7 3.1 copy.8
  169.8 136.3 %all-gather.5.cloned.1.call-done = f32[2,1024,1024]{2,1,0:T(8,128)} async-done(((f32[2,1024,256]{2,1,0:T(8,128)}), f32[2,1024,1024]{2,1,0:T(8,128)}) %all-gather.5.cloned.1.call-update) | async-done | bytes 8388624 | tf_op jit(solution)/shard_map/all_gather | solution.py:22
  306.3 89.2 %while.10 = (s32[]{:T(128)}, f32[1024,256]{0,1:T(8,128)S(1)}, f32[2,1024,256]{1,2,0:T(8,128)}, f32[2,1024,1024]{2,1,0:T(8,128)}, s32[]{:T(128)}) while((s32[]{:T(128)}, f32[1024,256]{0,1:T(8,128)S(1)}, f32[2,1024,256]{1,2,0:T(8,128)}, f32[2,1024,1024]{2,1,0:T(8,128)}, s32[]{:T(128)}) %tuple.20), condition=%wide.region_1.0_spmd, body=%wide.region_0.0_spmd.sunk | while | flops 6442975232 | bytes 27263104 | solution.py:38
  306.3 6.5 %fusion.40 = f32[1024,256]{0,1:T(8,128)S(1)} fusion(f32[1024,256]{0,1:T(8,128)S(1)} %get-tuple-element.75, f32[2,1024,1024]{2,1,0:T(8,128)} %get-tuple-element.82, f32[2,1024,256]{1,2,0:T(8,128)} %get-tuple-element.81), kind=kOutput, calls=%fused_computation.7.clone.1 | convolution fusion | flops 3221487616 | bytes 7340032 | tf_op jit(solution)/shard_map/while/body/eval_jaxpr/dot_general | solution.py:16
  312.8 6.9 %fusion.41 = f32[1024,256]{0,1:T(8,128)} fusion(f32[1024,256]{0,1:T(8,128)S(1)} %fusion.40, f32[2,1024,1024]{2,1,0:T(8,128)} %get-tuple-element.82, f32[2,1024,256]{1,2,0:T(8,128)S(1)} %copy-done.1), kind=kOutput, calls=%fused_computation.9.clone.1 | convolution fusion | flops 3221487616 | bytes 7340032 | tf_op jit(solution)/shard_map/while/body/eval_jaxpr/dot_general | solution.py:16
  319.7 2.4 collective-permute-start
  322.1 14.0 %collective-permute-done = f32[1024,256]{0,1:T(8,128)S(1)} collective-permute-done((f32[1024,256]{0,1:T(8,128)}, f32[1024,256]{0,1:T(8,128)S(1)}, u32[]{:S(2)}, u32[]{:S(2)}) %collective-permute-start) | collective-permute-done | bytes 1048608 | tf_op jit(solution)/shard_map/while/body/eval_jaxpr/ppermute | solution.py:12
  336.0 6.5 %fusion.40 = f32[1024,256]{0,1:T(8,128)S(1)} fusion(f32[1024,256]{0,1:T(8,128)S(1)} %get-tuple-element.75, f32[2,1024,1024]{2,1,0:T(8,128)} %get-tuple-element.82, f32[2,1024,256]{1,2,0:T(8,128)} %get-tuple-element.81), kind=kOutput, calls=%fused_computation.7.clone.1 | convolution fusion | flops 3221487616 | bytes 7340032 | tf_op jit(solution)/shard_map/while/body/eval_jaxpr/dot_general | solution.py:16
  342.5 6.9 %fusion.41 = f32[1024,256]{0,1:T(8,128)} fusion(f32[1024,256]{0,1:T(8,128)S(1)} %fusion.40, f32[2,1024,1024]{2,1,0:T(8,128)} %get-tuple-element.82, f32[2,1024,256]{1,2,0:T(8,128)S(1)} %copy-done.1), kind=kOutput, calls=%fused_computation.9.clone.1 | convolution fusion | flops 3221487616 | bytes 7340032 | tf_op jit(solution)/shard_map/while/body/eval_jaxpr/dot_general | solution.py:16
  349.4 1.9 collective-permute-start
  351.4 14.4 %collective-permute-done = f32[1024,256]{0,1:T(8,128)S(1)} collective-permute-done((f32[1024,256]{0,1:T(8,128)}, f32[1024,256]{0,1:T(8,128)S(1)}, u32[]{:S(2)}, u32[]{:S(2)}) %collective-permute-start) | collective-permute-done | bytes 1048608 | tf_op jit(solution)/shard_map/while/body/eval_jaxpr/ppermute | solution.py:12
  365.8 6.5 %fusion.40 = f32[1024,256]{0,1:T(8,128)S(1)} fusion(f32[1024,256]{0,1:T(8,128)S(1)} %get-tuple-element.75, f32[2,1024,1024]{2,1,0:T(8,128)} %get-tuple-element.82, f32[2,1024,256]{1,2,0:T(8,128)} %get-tuple-element.81), kind=kOutput, calls=%fused_computation.7.clone.1 | convolution fusion | flops 3221487616 | bytes 7340032 | tf_op jit(solution)/shard_map/while/body/eval_jaxpr/dot_general | solution.py:16
  372.3 6.9 %fusion.41 = f32[1024,256]{0,1:T(8,128)} fusion(f32[1024,256]{0,1:T(8,128)S(1)} %fusion.40, f32[2,1024,1024]{2,1,0:T(8,128)} %get-tuple-element.82, f32[2,1024,256]{1,2,0:T(8,128)S(1)} %copy-done.1), kind=kOutput, calls=%fused_computation.9.clone.1 | convolution fusion | flops 3221487616 | bytes 7340032 | tf_op jit(solution)/shard_map/while/body/eval_jaxpr/dot_general | solution.py:16
  379.2 1.9 collective-permute-start
  381.1 14.4 %collective-permute-done = f32[1024,256]{0,1:T(8,128)S(1)} collective-permute-done((f32[1024,256]{0,1:T(8,128)}, f32[1024,256]{0,1:T(8,128)S(1)}, u32[]{:S(2)}, u32[]{:S(2)}) %collective-permute-start) | collective-permute-done | bytes 1048608 | tf_op jit(solution)/shard_map/while/body/eval_jaxpr/ppermute | solution.py:12
  395.5 6.1 %fusion.18 = f32[1024,256]{1,0:T(8,128)S(1)} fusion(f32[1024,256]{0,1:T(8,128)S(1)} %get-tuple-element.27, f32[2,1024,1024]{2,1,0:T(8,128)} %get-tuple-element.87, f32[2,1024,256]{2,1,0:T(8,128)} %fusion.23), kind=kOutput, calls=%fused_computation.17 | convolution fusion | flops 3221487616 | bytes 7340032 | tf_op jit(solution)/shard_map/dot_general | solution.py:16
  401.6 5.3 %fusion.21 = f32[1,1024,256]{2,1,0:T(8,128)S(1)} fusion(f32[1024,256]{1,0:T(8,128)S(1)} %fusion.18, f32[2,1024,1024]{2,1,0:T(8,128)} %get-tuple-element.87, f32[2,1024,256]{2,1,0:T(8,128)S(1)} %copy-done.2), kind=kOutput, calls=%fused_computation.20 | convolution fusion | flops 3221487616 | bytes 7340032 | tf_op jit(solution)/shard_map/dot_general | solution.py:16
  407.1 2.9 copy.11
  410.0 10.5 %gather_fusion = f32[1024,2,256]{2,1,0:T(2,128)} fusion(f32[2,1024,256]{2,0,1:T(2,128)} %copy.11, s32[1024]{0:T(1024)S(1)} %fusion.22), kind=kCustom, calls=%fused_computation | custom fusion | bytes 4198400 | tf_op jit(solution)/shard_map/jit(_take)/gather | solution.py:40
  420.5 5.2 %select_bitcast_fusion = f32[2,1024,256]{2,0,1:T(2,128)S(1)} fusion(f32[1024,2,256]{2,1,0:T(2,128)} %gather_fusion, pred[1024]{0:T(1024)(128)(4,1)S(1)} %compare_and_fusion), kind=kLoop, calls=%fused_computation.15 | loop fusion | flops 524288 | bytes 4195328 | tf_op jit(solution)/shard_map/jit(_take)/select_n | solution.py:40
  425.7 1.5 copy.12
  (19 shorter events, 1.0 us)
Async XLA Ops:
  6.5 150.2 %copy-start = (f32[2,1024,256]{2,1,0:T(8,128)S(1)}, f32[2,1024,256]{2,1,0:T(8,128)}, u32[]{:S(2)}) copy-start(f32[2,1024,256]{2,1,0:T(8,128)} %param.6) | copy-start | bytes 6291460
  6.5 1.5 copy-start.3
  6.5 150.2 %all-gather.3.cloned.1.call-start = ((), (), s32[]{:S(2)}) async-start(), calls=%async_computation | async-start | bytes 10485760 | tf_op jit(solution)/shard_map/all_gather | solution.py:21
  7.3 298.9 %all-gather.5.cloned.1.call-start = ((), (), s32[]{:S(2)}) async-start(), calls=%async_computation.1 | async-start | bytes 10485760 | tf_op jit(solution)/shard_map/all_gather | solution.py:22
  306.3 6.5 %copy-start.1 = (f32[2,1024,256]{1,2,0:T(8,128)S(1)}, f32[2,1024,256]{1,2,0:T(8,128)}, u32[]{:S(2)}) copy-start(f32[2,1024,256]{1,2,0:T(8,128)} %get-tuple-element.81) | copy-start | bytes 6291460 | tf_op jit(solution)/shard_map/while
  319.7 16.3 %collective-permute-start = (f32[1024,256]{0,1:T(8,128)}, f32[1024,256]{0,1:T(8,128)S(1)}, u32[]{:S(2)}, u32[]{:S(2)}) collective-permute-start(f32[1024,256]{0,1:T(8,128)} %fusion.41), channel_id=1, source_target_pairs={{4,0},{8,4},{12,8},{5,1},{9,5},{13,9},{6,2},{10,6},{14,10},{7,3},{... | collective-permute-start | bytes 3145736 | tf_op jit(solution)/shard_map/while/body/eval_jaxpr/ppermute | solution.py:12
  336.0 6.5 %copy-start.1 = (f32[2,1024,256]{1,2,0:T(8,128)S(1)}, f32[2,1024,256]{1,2,0:T(8,128)}, u32[]{:S(2)}) copy-start(f32[2,1024,256]{1,2,0:T(8,128)} %get-tuple-element.81) | copy-start | bytes 6291460 | tf_op jit(solution)/shard_map/while
  349.4 16.3 %collective-permute-start = (f32[1024,256]{0,1:T(8,128)}, f32[1024,256]{0,1:T(8,128)S(1)}, u32[]{:S(2)}, u32[]{:S(2)}) collective-permute-start(f32[1024,256]{0,1:T(8,128)} %fusion.41), channel_id=1, source_target_pairs={{4,0},{8,4},{12,8},{5,1},{9,5},{13,9},{6,2},{10,6},{14,10},{7,3},{... | collective-permute-start | bytes 3145736 | tf_op jit(solution)/shard_map/while/body/eval_jaxpr/ppermute | solution.py:12
  365.8 6.5 %copy-start.1 = (f32[2,1024,256]{1,2,0:T(8,128)S(1)}, f32[2,1024,256]{1,2,0:T(8,128)}, u32[]{:S(2)}) copy-start(f32[2,1024,256]{1,2,0:T(8,128)} %get-tuple-element.81) | copy-start | bytes 6291460 | tf_op jit(solution)/shard_map/while
  379.2 16.3 %collective-permute-start = (f32[1024,256]{0,1:T(8,128)}, f32[1024,256]{0,1:T(8,128)S(1)}, u32[]{:S(2)}, u32[]{:S(2)}) collective-permute-start(f32[1024,256]{0,1:T(8,128)} %fusion.41), channel_id=1, source_target_pairs={{4,0},{8,4},{12,8},{5,1},{9,5},{13,9},{6,2},{10,6},{14,10},{7,3},{... | collective-permute-start | bytes 3145736 | tf_op jit(solution)/shard_map/while/body/eval_jaxpr/ppermute | solution.py:12
  395.5 6.1 %copy-start.2 = (f32[2,1024,256]{2,1,0:T(8,128)S(1)}, f32[2,1024,256]{2,1,0:T(8,128)}, u32[]{:S(2)}) copy-start(f32[2,1024,256]{2,1,0:T(8,128)} %fusion.23) | copy-start | bytes 6291460
Sparse Core Ops, SparseCore 0:
  8.9 147.7 all-gather.2
  158.3 147.8 all-gather.4

commit v2 on v1

v2 whole, which is shorter than its diff:
```python
import jax
import jax.numpy as jnp
from jax import lax
from jax.sharding import PartitionSpec as P

fast = lax.Precision.HIGH


def shifted(block, axis, distance):
    devices = range(lax.axis_size(axis))
    route = [(i - distance, i) for i in devices if i - distance in devices]
    return lax.ppermute(block, axis, route)


def apply(matrix, operand):
    return jnp.dot(matrix, operand, precision=fast, preferred_element_type=jnp.float32)


def shards(noise, inv_diag, coupling, order):
    block_count = noise.shape[0]
    sample_count = noise.shape[2]
    pieces = 2 if sample_count % 256 == 0 else 1
    width = sample_count // pieces
    inv_full = lax.all_gather(inv_diag, "cols", axis=2, tiled=True)
    coupling_full = [
        lax.all_gather(coupling[block], "cols", axis=1, tiled=True) for block in range(block_count)
    ]
    driven = jnp.einsum(
        "kmn,kns->kms", inv_full, noise, precision=fast, preferred_element_type=jnp.float32
    )
    driven_pieces = [
        [driven[block][:, p * width:(p + 1) * width] for p in range(pieces)]
        for block in range(block_count)
    ]

    def chain(entering, piece, skip_last):
        carried = entering
        results = [None] * block_count
        for block in range(block_count - 1, -1, -1):
            if skip_last and block == block_count - 1:
                carried = driven_pieces[block][piece]
            else:
                carried = driven_pieces[block][piece] + apply(coupling_full[block], carried)
            results[block] = carried
        return results

    first = [shifted(chain(None, p, True)[0], "tm", -1) for p in range(pieces)]

    def relay_step(step, entering):
        return [shifted(chain(entering[p], p, False)[0], "tm", -1) for p in range(pieces)]

    entering = lax.fori_loop(0, lax.axis_size("tm") - 2, relay_step, first)
    finals = [chain(entering[p], p, False) for p in range(pieces)]
    stacked = jnp.stack(
        [jnp.concatenate([finals[p][block] for p in range(pieces)], axis=1) for block in range(block_count)],
        axis=0,
    )
    return stacked.at[:, order].get(mode="promise_in_bounds")


def solution(mesh):
    return jax.shard_map(
        shards,
        mesh=mesh,
        in_specs=(
            P(("parts", "tm"), None, "cols"),
            P(("parts", "tm"), None, "cols"),
            P(("parts", "tm"), None, "cols"),
            P(),
        ),
        out_specs=P(("parts", "tm"), None, "cols"),
        check_vma=False,
    )
```

time: 439 us -> 415 us (0.945)
  waiting for transfers between devices: 329 us -> 302 us
  local copies, waits for them, and re-layouts: 18.1 us -> 26.7 us
  matrix products: 61.6 us -> 54.5 us
  starting transfers between devices: 6.21 us -> 12.9 us
    ppermute x3 -> x6, waiting for transfers between devices: 42.8 us -> 17.8 us  [shifted(): return lax.ppermute(block, axis, route)]
    dot_general x9 -> x15, matrix products: 61.6 us -> 54.5 us  [the longest x14 48.6 us: apply(): jnp.dot(matrix, operand, precision=fast, preferred_element_type=jnp.float32)]
    ppermute x3 -> x6, starting transfers between devices: 6.17 us -> 12.8 us  [shifted(): return lax.ppermute(block, axis, route)]
    slice x0 -> x3, local copies, waits for them, and re-layouts: none -> 6.2 us  [the longest x2 3.2 us: shards(): driven[block][:, p * width:(p + 1) * width]]
    select_n x1 -> x0, other arithmetic: 5.23 us -> none  [shards(): return jnp.take(stacked, order, axis=1)]
    gather x1 -> x2, local copies, waits for them, and re-layouts: 10.5 us -> 13.6 us  [shards(): return stacked.at[:, order].get(mode='promise_in_bounds')]
    all_gather x1 -> x2, waiting for transfers between devices: 136 us -> 137 us  [shards(): lax.all_gather(coupling[block], 'cols', axis=1, tiled=True)]
  transfers between devices with their start and end apart: 5 -> 9, of which waited for: 5 -> 7; matrix products, arithmetic and copies ran while one was open for 3% -> 9% of each run, Pallas kernels for 0% -> 0%
where the time goes in v2:
time: 415 us; the launch traced here: 411 us
  waiting for transfers between devices  302 us (73%)
  matrix products  54.5 us (13%)
  local copies, waits for them, and re-layouts  26.7 us (6%)
  between operations  13.3 us (3%)
  starting transfers between devices  12.9 us (3%)
    all_gather x1, waiting for transfers between devices, shards(): inv_full = lax.all_gather(inv_diag, 'cols', axis=2, tiled=True)  146 us
    all_gather x2, waiting for transfers between devices, shards(): lax.all_gather(coupling[block], 'cols', axis=1, tiled=True)  137 us
    dot_general x14, matrix products, apply(): jnp.dot(matrix, operand, precision=fast, preferred_element_type=jnp.float32)  48.6 us
    ppermute x6, waiting for transfers between devices, shifted(): return lax.ppermute(block, axis, route)  17.8 us
    gather x2, local copies, waits for them, and re-layouts, shards(): return stacked.at[:, order].get(mode='promise_in_bounds')  13.6 us
    ppermute x6, starting transfers between devices, shifted(): return lax.ppermute(block, axis, route)  12.8 us
  transfers between devices with their start and end apart: 9, of which 7 were waited for; matrix products, arithmetic and copies ran while one was open for 9% of the time, Pallas kernels for 0%

profile of v2, /device:TPU:25, one launch (start us, length us, event | category | flops | bytes accessed | tf_op | source)
XLA Modules:
  0.0 411.0 jit_solution(12295888507062016124)
XLA Ops:
  7.3 3.0 fusion.17
  11.1 145.6 %all-gather.6.cloned.1.call-done = f32[2,1024,1024]{2,1,0:T(8,128)} async-done(((f32[2,1024,256]{2,1,0:T(8,128)}), f32[2,1024,1024]{2,1,0:T(8,128)}) %all-gather.6.cloned.1.call-update) | async-done | bytes 8388624 | tf_op jit(solution)/shard_map/all_gather | solution.py:24
  156.7 5.9 %fusion.20 = f32[2,1024,256]{1,2,0:T(8,128)S(1)} fusion(f32[2,1024,1024]{2,1,0:T(8,128)} %all-gather.6.cloned.1.call-done, f32[2,1024,256]{2,1,0:T(8,128)S(1)} %copy-done), kind=kOutput, calls=%fused_computation.37 | convolution fusion | flops 3221225472 | bytes 12582912 | tf_op jit(solution)/shard_map/kmn,kns->kms/dot_general | solution.py:28
  163.8 73.8 %all-gather.8.cloned.1.call-done = f32[1,1024,1024]{2,1,0:T(8,128)} async-done(((f32[1,1024,256]{2,1,0:T(8,128)}), f32[1,1024,1024]{2,1,0:T(8,128)}) %all-gather.8.cloned.1.call-update) | async-done | bytes 4194320 | tf_op jit(solution)/shard_map/all_gather | solution.py:26
  237.6 5.5 %fusion.6 = f32[1024,128]{0,1:T(8,128)} fusion(f32[1,1024,1024]{2,1,0:T(8,128)} %all-gather.8.cloned.1.call-done, f32[1024,256]{0,1:T(8,128)} %get-tuple-element.94, f32[1024,256]{0,1:T(8,128)S(1)} %get-tuple-element.93), kind=kOutput, calls=%fused_computation.17 | convolution fusion | flops 805437440 | bytes 5767168 | tf_op jit(solution)/shard_map/dot_general | solution.py:16
  245.5 3.1 fusion.7
  255.4 63.2 %all-gather.10.cloned.1.call-done = f32[1,1024,1024]{2,1,0:T(8,128)} async-done(((f32[1,1024,256]{2,1,0:T(8,128)}), f32[1,1024,1024]{2,1,0:T(8,128)}) %all-gather.10.cloned.1.call-update) | async-done | bytes 4194320 | tf_op jit(solution)/shard_map/all_gather | solution.py:26
  318.5 53.5 %while.12 = (s32[]{:T(128)}, f32[1024,128]{0,1:T(8,128)}, f32[1024,128]{0,1:T(8,128)}, f32[1024,1024]{1,0:T(8,128)}, f32[1024,128]{1,0:T(8,128)S(1)}, /*index=5*...) while((s32[]{:T(128)}, f32[1024,128]{0,1:T(8,128)}, ...), condition=%wide.region_1.0_spmd, body=%wide.region_0.0_spmd.sunk | while | flops 3221749760 | bytes 65012004 | solution.py:52
  318.6 4.3 %convolution_add_fusion.4 = f32[1024,128]{1,0:T(8,128)S(1)} fusion(f32[1024,128]{1,0:T(8,128)S(1)} %get-tuple-element.180, f32[1024,1024]{1,0:T(8,128)} %get-tuple-element.179, f32[1024,128]{0,1:T(8,128)} %get-tuple-element.167), kind=kOutput, calls=%fused_computation.2.clone.1 | convolution fusion | flops 805437440 | bytes 5767168 | tf_op jit(solution)/shard_map/while/body/eval_jaxpr/dot_general | solution.py:16
  322.9 3.2 fusion.53
  326.1 2.5 collective-permute-start
  328.6 2.9 convolution_add_fusion.5
  331.5 3.2 fusion.54
  337.0 8.5 %collective-permute-done.1 = f32[1024,128]{0,1:T(8,128)} collective-permute-done((f32[1024,128]{0,1:T(8,128)}, f32[1024,128]{0,1:T(8,128)}, u32[]{:S(2)}, u32[]{:S(2)}) %collective-permute-start.1) | collective-permute-done | bytes 524320 | tf_op jit(solution)/shard_map/while/body/eval_jaxpr/ppermute | solution.py:12
  345.5 4.3 %convolution_add_fusion.4 = f32[1024,128]{1,0:T(8,128)S(1)} fusion(f32[1024,128]{1,0:T(8,128)S(1)} %get-tuple-element.180, f32[1024,1024]{1,0:T(8,128)} %get-tuple-element.179, f32[1024,128]{0,1:T(8,128)} %get-tuple-element.167), kind=kOutput, calls=%fused_computation.2.clone.1 | convolution fusion | flops 805437440 | bytes 5767168 | tf_op jit(solution)/shard_map/while/body/eval_jaxpr/dot_general | solution.py:16
  349.8 3.2 fusion.53
  355.1 2.9 convolution_add_fusion.5
  358.0 3.2 fusion.54
  364.0 8.0 %collective-permute-done.1 = f32[1024,128]{0,1:T(8,128)} collective-permute-done((f32[1024,128]{0,1:T(8,128)}, f32[1024,128]{0,1:T(8,128)}, u32[]{:S(2)}, u32[]{:S(2)}) %collective-permute-start.1) | collective-permute-done | bytes 524320 | tf_op jit(solution)/shard_map/while/body/eval_jaxpr/ppermute | solution.py:12
  372.0 4.8 %fusion.5 = f32[1024,128]{0,1:T(8,128)S(1)} fusion(f32[1024,128]{0,1:T(8,128)} %get-tuple-element.53, f32[1,1024,1024]{2,1,0:T(8,128)} %bitcast.93, f32[1024,256]{0,1:T(8,128)} %get-tuple-element.94), kind=kOutput, calls=%fused_computation.15 | convolution fusion | flops 805437440 | bytes 5767168 | tf_op jit(solution)/shard_map/dot_general | solution.py:16
  379.4 3.4 fusion.3
  386.8 4.1 %copy.12 = f32[2,1024,256]{2,0,1:T(2,128)} copy(f32[2,1024,256]{1,2,0:T(8,128)} %pad_maximum_fusion) | data formatting | bytes 4194304 | tf_op jit(solution)/shard_map/stack | solution.py:54
  390.9 10.5 %gather_fusion = f32[1024,2,256]{2,1,0:T(2,128)} fusion(f32[2,1024,256]{2,0,1:T(2,128)} %copy.12, s32[1024]{0:T(1024)S(1)} %fusion.8), kind=kCustom, calls=%fused_computation | custom fusion | bytes 4198400 | tf_op jit(solution)/shard_map/gather | solution.py:58
  401.4 3.1 copy.13
  (59 shorter events, 25.4 us)
Async XLA Ops:
  6.5 150.2 %copy-start = (f32[2,1024,256]{2,1,0:T(8,128)S(1)}, f32[2,1024,256]{2,1,0:T(8,128)}, u32[]{:S(2)}) copy-start(f32[2,1024,256]{2,1,0:T(8,128)} %param.6) | copy-start | bytes 6291460
  6.5 4.5 %copy-start.12 = (s32[1024]{0:T(1024)S(1)}, s32[1024]{0:T(1024)}, u32[]{:S(2)}) copy-start(s32[1024]{0:T(1024)} %param.9) | copy-start | bytes 12292
  6.5 150.2 %all-gather.6.cloned.1.call-start = ((), (), s32[]{:S(2)}) async-start(), calls=%async_computation | async-start | bytes 10485760 | tf_op jit(solution)/shard_map/all_gather | solution.py:24
  7.3 230.4 %all-gather.8.cloned.1.call-start = ((), (), s32[]{:S(2)}) async-start(), calls=%async_computation.1 | async-start | bytes 5242880 | tf_op jit(solution)/shard_map/all_gather | solution.py:26
  10.3 308.2 %all-gather.10.cloned.1.call-start = ((), (), s32[]{:S(2)}) async-start(), calls=%async_computation.2 | async-start | bytes 5242880 | tf_op jit(solution)/shard_map/all_gather | solution.py:26
  163.8 84.8 %copy-start.8 = (f32[1024,256]{0,1:T(8,128)}, f32[1024,256]{0,1:T(8,128)S(1)}, u32[]{:S(2)}) copy-start(f32[1024,256]{0,1:T(8,128)S(1)} %get-tuple-element.93) | copy-start | bytes 3145732
  237.6 7.9 %copy-start.1 = (f32[1,1024,1024]{2,1,0:T(8,128)S(1)}, f32[1,1024,1024]{2,1,0:T(8,128)}, u32[]{:S(2)}) copy-start(f32[1,1024,1024]{2,1,0:T(8,128)} %all-gather.8.cloned.1.call-done) | copy-start | bytes 12582916
  237.6 7.9 %copy-start.10 = (f32[1024,256]{0,1:T(8,128)S(1)}, f32[1024,256]{0,1:T(8,128)}, u32[]{:S(2)}) copy-start(f32[1024,256]{0,1:T(8,128)} %get-tuple-element.94) | copy-start | bytes 3145732
  243.1 75.4 %collective-permute-start.3 = (f32[1024,128]{0,1:T(8,128)}, f32[1024,128]{0,1:T(8,128)}, u32[]{:S(2)}, u32[]{:S(2)}) collective-permute-start(f32[1024,128]{0,1:T(8,128)} %fusion.6), channel_id=1, source_target_pairs={{4,0},{8,4},{12,8},{5,1},{9,5},{13,9},{6,2},{10,6},{14,10},{7,3},{... | collective-permute-start | bytes 1572872 | tf_op jit(solution)/shard_map/ppermute | solution.py:12
  248.6 69.9 %collective-permute-start.2 = (f32[1024,128]{0,1:T(8,128)}, f32[1024,128]{0,1:T(8,128)}, u32[]{:S(2)}, u32[]{:S(2)}) collective-permute-start(f32[1024,128]{0,1:T(8,128)} %fusion.7), channel_id=1, source_target_pairs={{4,0},{8,4},{12,8},{5,1},{9,5},{13,9},{6,2},{10,6},{14,10},{7,3},{... | collective-permute-start | bytes 1572872 | tf_op jit(solution)/shard_map/ppermute | solution.py:12
  318.5 4.3 %copy-start.2 = (f32[1024,1024]{1,0:T(8,128)S(1)}, f32[1024,1024]{1,0:T(8,128)}, u32[]{:S(2)}) copy-start(f32[1024,1024]{1,0:T(8,128)} %get-tuple-element.181) | copy-start | bytes 12582916 | tf_op jit(solution)/shard_map/while
  318.5 4.3 %copy-start.7 = (f32[1024,128]{0,1:T(8,128)S(1)}, f32[1024,128]{0,1:T(8,128)}, u32[]{:S(2)}) copy-start(f32[1024,128]{0,1:T(8,128)} %get-tuple-element.182) | copy-start | bytes 1572868 | tf_op jit(solution)/shard_map/while
  322.8 5.7 %copy-start.4 = (f32[1024,1024]{1,0:T(8,128)S(1)}, f32[1024,1024]{1,0:T(8,128)}, u32[]{:S(2)}) copy-start(f32[1024,1024]{1,0:T(8,128)} %get-tuple-element.179) | copy-start | bytes 12582916 | tf_op jit(solution)/shard_map/while
  326.1 5.4 %copy-start.6 = (f32[1024,128]{0,1:T(8,128)S(1)}, f32[1024,128]{0,1:T(8,128)}, u32[]{:S(2)}) copy-start(f32[1024,128]{0,1:T(8,128)} %get-tuple-element.184) | copy-start | bytes 1572868 | tf_op jit(solution)/shard_map/while
  326.1 11.0 %collective-permute-start = (f32[1024,128]{0,1:T(8,128)}, f32[1024,128]{0,1:T(8,128)}, u32[]{:S(2)}, u32[]{:S(2)}) collective-permute-start(f32[1024,128]{0,1:T(8,128)} %fusion.53), channel_id=1, source_target_pairs={{4,0},{8,4},{12,8},{5,1},{9,5},{13,9},{6,2},{10,6},{14,10},{7,3},{... | collective-permute-start | bytes 1572872 | tf_op jit(solution)/shard_map/while/body/eval_jaxpr/ppermute | solution.py:12
  334.7 10.8 %collective-permute-start.1 = (f32[1024,128]{0,1:T(8,128)}, f32[1024,128]{0,1:T(8,128)}, u32[]{:S(2)}, u32[]{:S(2)}) collective-permute-start(f32[1024,128]{0,1:T(8,128)} %fusion.54), channel_id=1, source_target_pairs={{4,0},{8,4},{12,8},{5,1},{9,5},{13,9},{6,2},{10,6},{14,10},{7,3},{... | collective-permute-start | bytes 1572872 | tf_op jit(solution)/shard_map/while/body/eval_jaxpr/ppermute | solution.py:12
  345.5 4.3 %copy-start.2 = (f32[1024,1024]{1,0:T(8,128)S(1)}, f32[1024,1024]{1,0:T(8,128)}, u32[]{:S(2)}) copy-start(f32[1024,1024]{1,0:T(8,128)} %get-tuple-element.181) | copy-start | bytes 12582916 | tf_op jit(solution)/shard_map/while
  345.5 4.3 %copy-start.7 = (f32[1024,128]{0,1:T(8,128)S(1)}, f32[1024,128]{0,1:T(8,128)}, u32[]{:S(2)}) copy-start(f32[1024,128]{0,1:T(8,128)} %get-tuple-element.182) | copy-start | bytes 1572868 | tf_op jit(solution)/shard_map/while
  349.8 5.3 %copy-start.4 = (f32[1024,1024]{1,0:T(8,128)S(1)}, f32[1024,1024]{1,0:T(8,128)}, u32[]{:S(2)}) copy-start(f32[1024,1024]{1,0:T(8,128)} %get-tuple-element.179) | copy-start | bytes 12582916 | tf_op jit(solution)/shard_map/while
  353.0 4.9 %copy-start.6 = (f32[1024,128]{0,1:T(8,128)S(1)}, f32[1024,128]{0,1:T(8,128)}, u32[]{:S(2)}) copy-start(f32[1024,128]{0,1:T(8,128)} %get-tuple-element.184) | copy-start | bytes 1572868 | tf_op jit(solution)/shard_map/while
  353.0 10.9 %collective-permute-start = (f32[1024,128]{0,1:T(8,128)}, f32[1024,128]{0,1:T(8,128)}, u32[]{:S(2)}, u32[]{:S(2)}) collective-permute-start(f32[1024,128]{0,1:T(8,128)} %fusion.53), channel_id=1, source_target_pairs={{4,0},{8,4},{12,8},{5,1},{9,5},{13,9},{6,2},{10,6},{14,10},{7,3},{... | collective-permute-start | bytes 1572872 | tf_op jit(solution)/shard_map/while/body/eval_jaxpr/ppermute | solution.py:12
  361.2 10.8 %collective-permute-start.1 = (f32[1024,128]{0,1:T(8,128)}, f32[1024,128]{0,1:T(8,128)}, u32[]{:S(2)}, u32[]{:S(2)}) collective-permute-start(f32[1024,128]{0,1:T(8,128)} %fusion.54), channel_id=1, source_target_pairs={{4,0},{8,4},{12,8},{5,1},{9,5},{13,9},{6,2},{10,6},{14,10},{7,3},{... | collective-permute-start | bytes 1572872 | tf_op jit(solution)/shard_map/while/body/eval_jaxpr/ppermute | solution.py:12
  372.0 4.8 %copy-start.3 = (f32[1024,1024]{1,0:T(8,128)S(1)}, f32[1024,1024]{1,0:T(8,128)}, u32[]{:S(2)}) copy-start(f32[1024,1024]{1,0:T(8,128)} %get-tuple-element.190) | copy-start | bytes 12582916
  372.0 4.8 %copy-start.9 = (f32[1024,256]{0,1:T(8,128)S(1)}, f32[1024,256]{0,1:T(8,128)}, u32[]{:S(2)}) copy-start(f32[1024,256]{0,1:T(8,128)} %copy-done.8) | copy-start | bytes 3145732
  (2 other events, 4.8 us)
Sparse Core Ops, SparseCore 0:
  8.9 147.7 all-gather.5
  158.3 79.2 all-gather.7
  239.2 79.2 all-gather.9

commit v3 on v2

v3 whole, which is shorter than its diff:
```python
import jax
import jax.numpy as jnp
from jax import lax
from jax.sharding import PartitionSpec as P

low = jnp.bfloat16


def shifted(block, axis, distance):
    devices = range(lax.axis_size(axis))
    route = [(i - distance, i) for i in devices if i - distance in devices]
    return lax.ppermute(block, axis, route)


def split(value, count):
    parts = []
    rest = value
    for index in range(count):
        kept = lax.reduce_precision(rest, exponent_bits=8, mantissa_bits=7)
        parts.append(kept.astype(low))
        if index < count - 1:
            rest = rest - kept
    return parts


def bdot(left, right):
    return jnp.dot(left, right, preferred_element_type=jnp.float32)


def apply(matrix_parts, operand):
    high, small = matrix_parts
    operand_high, operand_small = split(operand, 2)
    return bdot(high, operand_high) + (bdot(high, operand_small) + bdot(small, operand_high))


def shards(noise, inv_diag, coupling, order):
    block_count = noise.shape[0]
    node_count = noise.shape[1]
    sample_count = noise.shape[2]
    pieces = 2 if sample_count % 256 == 0 else 1
    width = sample_count // pieces
    inv_full = lax.all_gather(inv_diag, "cols", axis=2, tiled=True)
    coupling_parts = [
        split(lax.all_gather(coupling[block], "cols", axis=1, tiled=True), 2)
        for block in range(block_count)
    ]
    driven = [apply(split(inv_full[block], 2), noise[block]) for block in range(block_count)]
    driven_pieces = [
        [driven[block][:, p * width:(p + 1) * width] for p in range(pieces)]
        for block in range(block_count)
    ]

    def chain(entering, piece, skip_last):
        carried = entering
        results = [None] * block_count
        for block in range(block_count - 1, -1, -1):
            if skip_last and block == block_count - 1:
                carried = driven_pieces[block][piece]
            else:
                carried = driven_pieces[block][piece] + apply(coupling_parts[block], carried)
            results[block] = carried
        return results

    first = [shifted(chain(None, p, True)[0], "tm", -1) for p in range(pieces)]

    def relay_step(step, entering):
        return [shifted(chain(entering[p], p, False)[0], "tm", -1) for p in range(pieces)]

    entering = lax.fori_loop(0, lax.axis_size("tm") - 2, relay_step, first)
    finals = [chain(entering[p], p, False) for p in range(pieces)]
    selector = (order[:, None] == jnp.arange(node_count, dtype=order.dtype)[None, :]).astype(low)
    outputs = []
    for block in range(block_count):
        field = jnp.concatenate([finals[p][block] for p in range(pieces)], axis=1)
        top, middle, bottom = split(field, 3)
        outputs.append(bdot(selector, top) + (bdot(selector, middle) + bdot(selector, bottom)))
    return jnp.stack(outputs, axis=0)


def solution(mesh):
    return jax.shard_map(
        shards,
        mesh=mesh,
        in_specs=(
            P(("parts", "tm"), None, "cols"),
            P(("parts", "tm"), None, "cols"),
            P(("parts", "tm"), None, "cols"),
            P(),
        ),
        out_specs=P(("parts", "tm"), None, "cols"),
        check_vma=False,
    )
```

time: 415 us -> 440 us (1.060)
  waiting for transfers between devices: 302 us -> 322 us
  local copies, waits for them, and re-layouts: 26.7 us -> 16.8 us
  other arithmetic: 1.71 us -> 10.9 us
  matrix products: 54.5 us -> 59.5 us
    all_gather x2, waiting for transfers between devices: 137 us -> 154 us  [shards(): lax.all_gather(coupling[block], 'cols', axis=1, tiled=True)]
    gather x2 -> x0, local copies, waits for them, and re-layouts: 13.6 us -> none  [shards(): return stacked.at[:, order].get(mode='promise_in_bounds')]
    convert_element_type x0 -> x2, other arithmetic: none -> 9.48 us  [split(): parts.append(kept.astype(low))]
    dot_general x15 -> x54, matrix products: 54.5 us -> 59.5 us  [bdot(): return jnp.dot(left, right, preferred_element_type=jnp.float32)]
  transfers between devices with their start and end apart: 9 -> 9, of which waited for: 7 -> 8; matrix products, arithmetic and copies ran while one was open for 9% -> 6% of each run, Pallas kernels for 0% -> 0%
where the time goes in v3:
time: 440 us; the launch traced here: 435 us
  waiting for transfers between devices  322 us (73%)
  matrix products  59.5 us (14%)
  local copies, waits for them, and re-layouts  16.8 us (4%)
  between operations  13.4 us (3%)
  starting transfers between devices  12.2 us (3%)
  other arithmetic  10.9 us (2%)
    all_gather x2, waiting for transfers between devices, shards(): lax.all_gather(coupling[block], 'cols', axis=1, tiled=True)  154 us
    all_gather x1, waiting for transfers between devices, shards(): inv_full = lax.all_gather(inv_diag, 'cols', axis=2, tiled=True)  144 us
    dot_general x54, matrix products, bdot(): return jnp.dot(left, right, preferred_element_type=jnp.float32)  59.5 us
    ppermute x6, waiting for transfers between devices, shifted(): return lax.ppermute(block, axis, route)  22 us
    ppermute x6, starting transfers between devices, shifted(): return lax.ppermute(block, axis, route)  12.1 us
    convert_element_type x2, other arithmetic, split(): parts.append(kept.astype(low))  9.48 us
  transfers between devices with their start and end apart: 9, of which 8 were waited for; matrix products, arithmetic and copies ran while one was open for 6% of the time, Pallas kernels for 0%

profile of v3, /device:TPU:25, one launch (start us, length us, event | category | flops | bytes accessed | tf_op | source)
XLA Modules:
  0.0 435.3 jit_solution(6839977181822519246)
XLA Ops:
  6.5 3.0 fusion.150
  11.0 77.9 %all-gather.8.cloned.1.call-done = f32[1,1024,1024]{2,1,0:T(8,128)} async-done(((f32[1,1024,256]{2,1,0:T(8,128)}), f32[1,1024,1024]{2,1,0:T(8,128)}) %all-gather.8.cloned.1.call-update) | async-done | bytes 4194320 | tf_op jit(solution)/shard_map/all_gather | solution.py:44
  88.9 4.4 %reduce-precision_convert_fusion.13 = (bf16[1024,1024]{1,0:T(8,128)(2,1)S(1)}, bf16[1024,1024]{1,0:T(8,128)(2,1)}) fusion(f32[1,1024,1024]{2,1,0:T(8,128)} %all-gather.8.cloned.1.call-done), kind=kLoop, calls=%fused_computation.43 | loop fusion | flops 5242880 | bytes 8388608 | tf_op jit(solution)/shard_map/convert_element_type | solution.py:20
  93.4 76.5 %all-gather.10.cloned.1.call-done = f32[1,1024,1024]{2,1,0:T(8,128)} async-done(((f32[1,1024,256]{2,1,0:T(8,128)}), f32[1,1024,1024]{2,1,0:T(8,128)}) %all-gather.10.cloned.1.call-update) | async-done | bytes 4194320 | tf_op jit(solution)/shard_map/all_gather | solution.py:44
  169.8 5.0 %reduce-precision_convert_fusion.12 = (bf16[1024,1024]{1,0:T(8,128)(2,1)}, bf16[1024,1024]{1,0:T(8,128)(2,1)}) fusion(f32[1,1024,1024]{2,1,0:T(8,128)} %all-gather.10.cloned.1.call-done), kind=kLoop, calls=%fused_computation.41 | loop fusion | flops 5242880 | bytes 8388608 | tf_op jit(solution)/shard_map/convert_element_type | solution.py:20
  174.9 144.4 %all-gather.6.cloned.1.call-done = f32[2,1024,1024]{2,1,0:T(8,128)} async-done(((f32[2,1024,256]{2,1,0:T(8,128)}), f32[2,1024,1024]{2,1,0:T(8,128)}) %all-gather.6.cloned.1.call-update) | async-done | bytes 8388624 | tf_op jit(solution)/shard_map/all_gather | solution.py:42
  319.3 3.4 fusion.47
  322.7 3.8 fusion.97
  337.3 2.4 collective-permute-start.2
  339.7 2.1 collective-permute-start.3
  342.8 2.0 copy.10
  344.9 2.0 copy.9
  346.9 2.3 fusion.151
  349.2 4.4 %collective-permute-done.3 = f32[1024,128]{0,1:T(8,128)S(1)} collective-permute-done((f32[1024,128]{0,1:T(8,128)}, f32[1024,128]{0,1:T(8,128)S(1)}, u32[]{:S(2)}, u32[]{:S(2)}) %collective-permute-start.3) | collective-permute-done | bytes 524320 | tf_op jit(solution)/shard_map/ppermute | solution.py:12
  353.6 54.2 %while.12 = (s32[]{:T(128)}, f32[1024,128]{0,1:T(8,128)S(1)}, f32[1024,128]{0,1:T(8,128)S(1)}, bf16[1024,1024]{1,0:T(8,128)(2,1)}, bf16[1024,1024]{1,0:T(8,128)(...) while((s32[]{:T(128)}, f32[1024,128]{0,1:T(8,128)S(1)}, ...), condition=%wide.region_1.0_spmd, body=%wide.region_0.0_spmd.sunk | while | flops 3226992640 | bytes 81789320 | solution.py:69
  353.6 2.5 fusion.228
  362.0 1.9 collective-permute-start
  370.1 1.9 collective-permute-start.1
  372.7 8.0 %collective-permute-done.1 = f32[1024,128]{0,1:T(8,128)S(1)} collective-permute-done((f32[1024,128]{0,1:T(8,128)}, f32[1024,128]{0,1:T(8,128)S(1)}, u32[]{:S(2)}, u32[]{:S(2)}) %collective-permute-start.1) | collective-permute-done | bytes 524320 | tf_op jit(solution)/shard_map/while/body/eval_jaxpr/ppermute | solution.py:12
  380.8 2.5 fusion.228
  389.2 1.9 collective-permute-start
  397.2 1.9 collective-permute-start.1
  399.9 8.0 %collective-permute-done.1 = f32[1024,128]{0,1:T(8,128)S(1)} collective-permute-done((f32[1024,128]{0,1:T(8,128)}, f32[1024,128]{0,1:T(8,128)S(1)}, u32[]{:S(2)}, u32[]{:S(2)}) %collective-permute-start.1) | collective-permute-done | bytes 524320 | tf_op jit(solution)/shard_map/while/body/eval_jaxpr/ppermute | solution.py:12
  407.9 2.6 fusion.136
  (110 shorter events, 56.8 us)
Async XLA Ops:
  6.5 82.4 %all-gather.8.cloned.1.call-start = ((), (), s32[]{:S(2)}) async-start(), calls=%async_computation.1 | async-start | bytes 5242880 | tf_op jit(solution)/shard_map/all_gather | solution.py:44
  9.6 160.3 %all-gather.10.cloned.1.call-start = ((), (), s32[]{:S(2)}) async-start(), calls=%async_computation.2 | async-start | bytes 5242880 | tf_op jit(solution)/shard_map/all_gather | solution.py:44
  10.3 309.0 %all-gather.6.cloned.1.call-start = ((), (), s32[]{:S(2)}) async-start(), calls=%async_computation | async-start | bytes 10485760 | tf_op jit(solution)/shard_map/all_gather | solution.py:42
  319.3 7.2 %copy-start.7 = (f32[2,1024,1024]{2,1,0:T(8,128)S(1)}, f32[2,1024,1024]{2,1,0:T(8,128)}, u32[]{:S(2)}) copy-start(f32[2,1024,1024]{2,1,0:T(8,128)} %all-gather.6.cloned.1.call-done) | copy-start | bytes 25165828
  322.7 4.0 copy-start.14
  327.4 14.3 %copy-start.8 = (f32[1024,256]{0,1:T(8,128)}, f32[1024,256]{0,1:T(8,128)S(1)}, u32[]{:S(2)}) copy-start(f32[1024,256]{0,1:T(8,128)S(1)} %fusion.69) | copy-start | bytes 3145732
  333.9 1.7 copy-start.15
  337.3 11.9 %collective-permute-start.2 = (f32[1024,128]{0,1:T(8,128)}, f32[1024,128]{0,1:T(8,128)S(1)}, u32[]{:S(2)}, u32[]{:S(2)}) collective-permute-start(f32[1024,128]{0,1:T(8,128)} %fusion.71), channel_id=1, source_target_pairs={{4,0},{8,4},{12,8},{5,1},{9,5},{13,9},{6,2},{10,6},{14,10},{7,3},{... | collective-permute-start | bytes 1572872 | tf_op jit(solution)/shard_map/ppermute | solution.py:12
  339.7 14.0 %collective-permute-start.3 = (f32[1024,128]{0,1:T(8,128)}, f32[1024,128]{0,1:T(8,128)S(1)}, u32[]{:S(2)}, u32[]{:S(2)}) collective-permute-start(f32[1024,128]{0,1:T(8,128)} %fusion.74), channel_id=1, source_target_pairs={{4,0},{8,4},{12,8},{5,1},{9,5},{13,9},{6,2},{10,6},{14,10},{7,3},{... | collective-permute-start | bytes 1572872 | tf_op jit(solution)/shard_map/ppermute | solution.py:12
  353.6 2.5 copy-start
  358.7 1.6 copy-start.3
  358.7 1.7 copy-start.13
  360.4 3.6 copy-start.5
  362.0 10.7 %collective-permute-start = (f32[1024,128]{0,1:T(8,128)}, f32[1024,128]{0,1:T(8,128)S(1)}, u32[]{:S(2)}, u32[]{:S(2)}) collective-permute-start(f32[1024,128]{0,1:T(8,128)} %fusion.232), channel_id=1, source_target_pairs={{4,0},{8,4},{12,8},{5,1},{9,5},{13,9},{6,2},{10,6},{14,10},{7,3},{... | collective-permute-start | bytes 1572872 | tf_op jit(solution)/shard_map/while/body/eval_jaxpr/ppermute | solution.py:12
  370.1 10.7 %collective-permute-start.1 = (f32[1024,128]{0,1:T(8,128)}, f32[1024,128]{0,1:T(8,128)S(1)}, u32[]{:S(2)}, u32[]{:S(2)}) collective-permute-start(f32[1024,128]{0,1:T(8,128)} %fusion.238), channel_id=1, source_target_pairs={{4,0},{8,4},{12,8},{5,1},{9,5},{13,9},{6,2},{10,6},{14,10},{7,3},{... | collective-permute-start | bytes 1572872 | tf_op jit(solution)/shard_map/while/body/eval_jaxpr/ppermute | solution.py:12
  380.8 2.5 copy-start
  385.8 1.6 copy-start.3
  385.8 1.7 copy-start.13
  387.5 3.6 copy-start.5
  389.2 10.7 %collective-permute-start = (f32[1024,128]{0,1:T(8,128)}, f32[1024,128]{0,1:T(8,128)S(1)}, u32[]{:S(2)}, u32[]{:S(2)}) collective-permute-start(f32[1024,128]{0,1:T(8,128)} %fusion.232), channel_id=1, source_target_pairs={{4,0},{8,4},{12,8},{5,1},{9,5},{13,9},{6,2},{10,6},{14,10},{7,3},{... | collective-permute-start | bytes 1572872 | tf_op jit(solution)/shard_map/while/body/eval_jaxpr/ppermute | solution.py:12
  397.2 10.7 %collective-permute-start.1 = (f32[1024,128]{0,1:T(8,128)}, f32[1024,128]{0,1:T(8,128)S(1)}, u32[]{:S(2)}, u32[]{:S(2)}) collective-permute-start(f32[1024,128]{0,1:T(8,128)} %fusion.238), channel_id=1, source_target_pairs={{4,0},{8,4},{12,8},{5,1},{9,5},{13,9},{6,2},{10,6},{14,10},{7,3},{... | collective-permute-start | bytes 1572872 | tf_op jit(solution)/shard_map/while/body/eval_jaxpr/ppermute | solution.py:12
  407.9 2.6 copy-start.6
  410.4 1.6 copy-start.1
  415.0 1.6 copy-start.4
  (10 other events, 11.2 us)
Sparse Core Ops, SparseCore 0:
  9.7 79.2 all-gather.7
  90.5 79.2 all-gather.9
  171.4 147.8 all-gather.5

commit v4 on v3

v4 whole, which is shorter than its diff:
```python
import jax
import jax.numpy as jnp
from jax import lax
from jax.sharding import PartitionSpec as P

low = jnp.bfloat16


def shifted(block, axis, distance):
    devices = range(lax.axis_size(axis))
    route = [(i - distance, i) for i in devices if i - distance in devices]
    return lax.ppermute(block, axis, route)


def split(value, count):
    parts = []
    rest = value
    for index in range(count):
        kept = lax.reduce_precision(rest, exponent_bits=8, mantissa_bits=7)
        parts.append(kept.astype(low))
        if index < count - 1:
            rest = rest - kept
    return parts


def bdot(left, right):
    return jnp.dot(left, right, preferred_element_type=jnp.float32)


def apply(matrix_parts, operand):
    high, small = matrix_parts
    width = operand.shape[1]
    operand_high, operand_small = split(operand, 2)
    both = bdot(high, jnp.concatenate([operand_high, operand_small], axis=1))
    return both[:, :width] + (both[:, width:] + bdot(small, operand_high))


def gathered(tile, after):
    tile, _ = lax.optimization_barrier((tile, after))
    return lax.all_gather(tile, "cols", axis=tile.ndim - 1, tiled=True)


def shards(noise, inv_diag, coupling, order):
    block_count = noise.shape[0]
    node_count = noise.shape[1]
    sample_count = noise.shape[2]
    inv_full = lax.all_gather(inv_diag, "cols", axis=2, tiled=True)
    coupling_parts = []
    previous = inv_full
    for block in range(block_count):
        previous = gathered(coupling[block], previous)
        coupling_parts.append(split(previous, 2))
    driven = [apply(split(inv_full[block], 2), noise[block]) for block in range(block_count)]

    def chain(entering, skip_last):
        carried = entering
        results = [None] * block_count
        for block in range(block_count - 1, -1, -1):
            if skip_last and block == block_count - 1:
                carried = driven[block]
            else:
                carried = driven[block] + apply(coupling_parts[block], carried)
            results[block] = carried
        return results

    first = shifted(chain(None, True)[0], "tm", -1)

    def relay_step(step, entering):
        return shifted(chain(entering, False)[0], "tm", -1)

    entering = lax.fori_loop(0, lax.axis_size("tm") - 2, relay_step, first)
    finals = chain(entering, False)
    selector = (order[:, None] == jnp.arange(node_count, dtype=order.dtype)[None, :]).astype(low)
    outputs = []
    for block in range(block_count):
        picked = bdot(selector, jnp.concatenate(split(finals[block], 3), axis=1))
        top = picked[:, :sample_count]
        middle = picked[:, sample_count:2 * sample_count]
        bottom = picked[:, 2 * sample_count:]
        outputs.append(top + (middle + bottom))
    return jnp.stack(outputs, axis=0)


def solution(mesh):
    return jax.shard_map(
        shards,
        mesh=mesh,
        in_specs=(
            P(("parts", "tm"), None, "cols"),
            P(("parts", "tm"), None, "cols"),
            P(("parts", "tm"), None, "cols"),
            P(),
        ),
        out_specs=P(("parts", "tm"), None, "cols"),
        check_vma=False,
    )
```

time: 440 us -> 398 us (0.905)
  matrix products: 59.5 us -> 32.3 us
  local copies, waits for them, and re-layouts: 16.8 us -> 8.04 us
  starting transfers between devices: 12.2 us -> 6.93 us
    dot_general x54 -> x20, matrix products: 59.5 us -> 32.3 us  [bdot(): return jnp.dot(left, right, preferred_element_type=jnp.float32)]
    all_gather x2, waiting for transfers between devices: 154 us -> 144 us  [gathered(): return lax.all_gather(tile, 'cols', axis=tile.ndim - 1, tiled=True)]
    ppermute x6 -> x3, waiting for transfers between devices: 22 us -> 28.6 us  [shifted(): return lax.ppermute(block, axis, route)]
    slice x3 -> x0, local copies, waits for them, and re-layouts: 6.34 us -> none  [the longest x2 3.34 us: shards(): driven[block][:, p * width:(p + 1) * width]]
    ppermute x6 -> x3, starting transfers between devices: 12.1 us -> 6.85 us  [shifted(): return lax.ppermute(block, axis, route)]
    convert_element_type x2 -> x6, other arithmetic: 9.48 us -> 10.9 us  [split(): parts.append(kept.astype(low))]
  transfers between devices with their start and end apart: 9 -> 6, of which waited for: 8 -> 5; matrix products, arithmetic and copies ran while one was open for 6% -> 5% of each run, Pallas kernels for 0% -> 0%
where the time goes in v4:
time: 398 us; the launch traced here: 394 us
  waiting for transfers between devices  320 us (80%)
  matrix products  32.3 us (8%)
  between operations  13.3 us (3%)
  other arithmetic  12.8 us (3%)
  local copies, waits for them, and re-layouts  8.04 us (2%)
  starting transfers between devices  6.93 us (2%)
    all_gather x1, waiting for transfers between devices, shards(): inv_full = lax.all_gather(inv_diag, 'cols', axis=2, tiled=True)  147 us
    all_gather x2, waiting for transfers between devices, gathered(): return lax.all_gather(tile, 'cols', axis=tile.ndim - 1, tiled=True)  144 us
    dot_general x20, matrix products, bdot(): return jnp.dot(left, right, preferred_element_type=jnp.float32)  32.3 us
    ppermute x3, waiting for transfers between devices, shifted(): return lax.ppermute(block, axis, route)  28.6 us
    convert_element_type x6, other arithmetic, split(): parts.append(kept.astype(low))  10.9 us
  transfers between devices with their start and end apart: 6, of which 5 were waited for; matrix products, arithmetic and copies ran while one was open for 5% of the time, Pallas kernels for 0%

profile of v4, /device:TPU:25, one launch (start us, length us, event | category | flops | bytes accessed | tf_op | source)
XLA Modules:
  0.0 393.5 jit_solution(10623728900484825088)
XLA Ops:
  8.1 1.5 slice_bitcast_fusion.1
  9.6 147.1 %all-gather.4.cloned.1.call-done = f32[2,1024,1024]{2,1,0:T(8,128)} async-done(((f32[2,1024,256]{2,1,0:T(8,128)}), f32[2,1024,1024]{2,1,0:T(8,128)}) %all-gather.4.cloned.1.call-update) | async-done | bytes 8388624 | tf_op jit(solution)/shard_map/all_gather | solution.py:47
  156.8 80.8 %all-gather.6.cloned.1.call-done = f32[1024,1024]{1,0:T(8,128)} async-done(((f32[1024,256]{1,0:T(8,128)}), f32[1024,1024]{1,0:T(8,128)}) %all-gather.6.cloned.1.call-update) | async-done | bytes 4194320 | tf_op jit(solution)/shard_map/all_gather | solution.py:40
  238.0 3.7 fusion.44
  241.7 3.7 fusion.41
  246.2 1.9 fusion.80
  251.2 1.9 fusion.62
  253.1 2.6 collective-permute-start.1
  255.7 62.8 %all-gather.8.cloned.1.call-done = f32[1024,1024]{1,0:T(8,128)} async-done(((f32[1024,256]{1,0:T(8,128)}), f32[1024,1024]{1,0:T(8,128)}) %all-gather.8.cloned.1.call-update) | async-done | bytes 4194320 | tf_op jit(solution)/shard_map/all_gather | solution.py:40
  318.5 5.1 %reduce-precision_convert_fusion.2 = (bf16[1024,1024]{1,0:T(8,128)(2,1)}, bf16[1024,1024]{1,0:T(8,128)(2,1)}) fusion(f32[1024,1024]{1,0:T(8,128)} %all-gather.8.cloned.1.call-done), kind=kLoop, calls=%fused_computation.26 | loop fusion | flops 5242880 | bytes 8388608 | tf_op jit(solution)/shard_map/convert_element_type | solution.py:20
  323.7 49.8 %while.10 = (s32[]{:T(128)}, f32[1024,256]{0,1:T(8,128)}, bf16[1024,1024]{1,0:T(8,128)(2,1)}, bf16[1024,1024]{1,0:T(8,128)(2,1)}, f32[1024,256]{0,1:T(8,128)}, /...) while((s32[]{:T(128)}, f32[1024,256]{0,1:T(8,128)}, ...), condition=%wide.region_1.0_spmd, body=%wide.region_0.0_spmd.sunk | while | flops 3229614080 | bytes 59769076 | solution.py:71
  323.7 1.6 fusion.154
  330.3 1.8 fusion.156
  332.1 2.4 collective-permute-start
  334.5 14.1 %collective-permute-done = f32[1024,256]{0,1:T(8,128)} collective-permute-done((f32[1024,256]{0,1:T(8,128)}, f32[1024,256]{0,1:T(8,128)}, u32[]{:S(2)}, u32[]{:S(2)}) %collective-permute-start) | collective-permute-done | bytes 1048608 | tf_op jit(solution)/shard_map/while/body/eval_jaxpr/ppermute | solution.py:12
  348.6 1.6 fusion.154
  350.5 1.3 convolution_bitcast_fusion.5
  355.2 1.8 fusion.156
  357.0 1.9 collective-permute-start
  359.0 14.5 %collective-permute-done = f32[1024,256]{0,1:T(8,128)} collective-permute-done((f32[1024,256]{0,1:T(8,128)}, f32[1024,256]{0,1:T(8,128)}, u32[]{:S(2)}, u32[]{:S(2)}) %collective-permute-start) | collective-permute-done | bytes 1048608 | tf_op jit(solution)/shard_map/while/body/eval_jaxpr/ppermute | solution.py:12
  373.5 1.6 fusion.82
  381.1 2.0 fusion.25
  383.1 2.0 fusion.26
  385.6 1.5 pad_maximum_fusion
  (60 shorter events, 21.2 us)
Async XLA Ops:
  6.5 1.6 copy-start.6
  6.5 150.2 %all-gather.4.cloned.1.call-start = ((), (), s32[]{:S(2)}) async-start(), calls=%async_computation | async-start | bytes 10485760 | tf_op jit(solution)/shard_map/all_gather | solution.py:47
  7.3 230.4 %all-gather.6.cloned.1.call-start = ((), (), s32[]{:S(2)}) async-start(), calls=%async_computation.1 | async-start | bytes 5242880 | tf_op jit(solution)/shard_map/all_gather | solution.py:40
  9.6 228.1 %copy-start.4 = (f32[2,1024,256]{2,1,0:T(8,128)S(1)}, f32[2,1024,256]{2,1,0:T(8,128)}, u32[]{:S(2)}) copy-start(f32[2,1024,256]{2,1,0:T(8,128)} %param.6) | copy-start | bytes 6291460
  156.7 161.8 %all-gather.8.cloned.1.call-start = ((), (), s32[]{:S(2)}) async-start(), calls=%async_computation.2 | async-start | bytes 5242880 | tf_op jit(solution)/shard_map/all_gather | solution.py:40
  238.0 7.3 %slice-start = ((s8[8388608]{0:T(1024)(128)(4,1)}), s8[4194304]{0:T(1024)(128)(4,1)S(1)}, s32[]{:S(2)}) async-start(s8[8388608]{0:T(1024)(128)(4,1)} %bitcast.97), calls=%async_computation.3 | async-start | bytes 8388608
  241.7 3.7 slice-start.1
  246.2 2.9 copy-start.5
  249.8 1.4 copy-start.7
  253.1 70.6 %collective-permute-start.1 = (f32[1024,256]{0,1:T(8,128)}, f32[1024,256]{0,1:T(8,128)}, u32[]{:S(2)}, u32[]{:S(2)}) collective-permute-start(f32[1024,256]{0,1:T(8,128)} %fusion.62), channel_id=1, source_target_pairs={{4,0},{8,4},{12,8},{5,1},{9,5},{13,9},{6,2},{10,6},{14,10},{7,3},{... | collective-permute-start | bytes 3145736 | tf_op jit(solution)/shard_map/ppermute | solution.py:12
  323.7 1.9 copy-start.10
  325.6 1.6 copy-start
  325.6 1.9 copy-start.2
  327.4 1.6 copy-start.8
  332.1 16.5 %collective-permute-start = (f32[1024,256]{0,1:T(8,128)}, f32[1024,256]{0,1:T(8,128)}, u32[]{:S(2)}, u32[]{:S(2)}) collective-permute-start(f32[1024,256]{0,1:T(8,128)} %fusion.156), channel_id=1, source_target_pairs={{4,0},{8,4},{12,8},{5,1},{9,5},{13,9},{6,2},{10,6},{14,10},{7,3},{... | collective-permute-start | bytes 3145736 | tf_op jit(solution)/shard_map/while/body/eval_jaxpr/ppermute | solution.py:12
  348.6 1.9 copy-start.10
  350.5 1.6 copy-start
  350.5 1.9 copy-start.2
  352.3 1.6 copy-start.8
  357.0 16.4 %collective-permute-start = (f32[1024,256]{0,1:T(8,128)}, f32[1024,256]{0,1:T(8,128)}, u32[]{:S(2)}, u32[]{:S(2)}) collective-permute-start(f32[1024,256]{0,1:T(8,128)} %fusion.156), channel_id=1, source_target_pairs={{4,0},{8,4},{12,8},{5,1},{9,5},{13,9},{6,2},{10,6},{14,10},{7,3},{... | collective-permute-start | bytes 3145736 | tf_op jit(solution)/shard_map/while/body/eval_jaxpr/ppermute | solution.py:12
  373.5 1.9 copy-start.11
  375.4 1.6 copy-start.1
  375.4 1.9 copy-start.3
  377.2 1.6 copy-start.9
  (1 other events, 1.0 us)
Sparse Core Ops, SparseCore 0:
  8.9 147.7 all-gather.3
  158.3 79.2 all-gather.5
  239.2 79.2 all-gather.7

commit v5 on v4

--- a/solution.py
+++ b/solution.py
@@ -35,22 +35,37 @@
     return both[:, :width] + (both[:, width:] + bdot(small, operand_high))
 
 
-def gathered(tile, after):
-    tile, _ = lax.optimization_barrier((tile, after))
-    return lax.all_gather(tile, "cols", axis=tile.ndim - 1, tiled=True)
+def line_reduce_scatter(partial, axis):
+    count = lax.axis_size(axis)
+    me = lax.axis_index(axis)
+    width = partial.shape[2] // count
+
+    def tile(owner):
+        owner = jnp.clip(owner, 0, count - 1)
+        return lax.dynamic_slice_in_dim(partial, owner * width, width, axis=2)
+
+    rightward = jnp.zeros_like(tile(me))
+    leftward = jnp.zeros_like(tile(me))
+    for step in range(1, count):
+        right_route = [(k, k + 1) for k in range(0, min(step, count - 1))]
+        left_route = [(k, k - 1) for k in range(max(count - step, 1), count)]
+        rightward = lax.ppermute(tile(me + count - step) + rightward, axis, right_route)
+        leftward = lax.ppermute(tile(me - count + step) + leftward, axis, left_route)
+    return tile(me) + (rightward + leftward)
 
 
 def shards(noise, inv_diag, coupling, order):
     block_count = noise.shape[0]
     node_count = noise.shape[1]
     sample_count = noise.shape[2]
-    inv_full = lax.all_gather(inv_diag, "cols", axis=2, tiled=True)
-    coupling_parts = []
-    previous = inv_full
-    for block in range(block_count):
-        previous = gathered(coupling[block], previous)
-        coupling_parts.append(split(previous, 2))
-    driven = [apply(split(inv_full[block], 2), noise[block]) for block in range(block_count)]
+    coupling_full = lax.all_gather(coupling, "cols", axis=2, tiled=True)
+    noise_rows = lax.all_to_all(noise, "cols", 1, 2, tiled=True)
+    partial = jnp.stack(
+        [apply(split(inv_diag[block], 2), noise_rows[block]) for block in range(block_count)], axis=0
+    )
+    driven_all = line_reduce_scatter(partial, "cols")
+    driven = [driven_all[block] for block in range(block_count)]
+    coupling_parts = [split(coupling_full[block], 2) for block in range(block_count)]
 
     def chain(entering, skip_last):
         carried = entering

time: 398 us -> 434 us (1.090)
  starting transfers between devices: 6.93 us -> 46.6 us
  waiting for transfers between devices: 320 us -> 292 us
  other arithmetic: 12.8 us -> 28.9 us
  local copies, waits for them, and re-layouts: 8.04 us -> 22.7 us
  matrix products: 32.3 us -> 25.2 us
    all_gather x3 -> x1, waiting for transfers between devices: 291 us -> 0.02 us  [shards(): coupling_full = lax.all_gather(coupling, 'cols', axis=2, tiled=True)]
    ppermute x0 -> x6, waiting for transfers between devices: none -> 173 us  [the longest x3 135 us: line_reduce_scatter(): lax.ppermute(tile(me - count + step) + leftward, axis, left_route)]
    all_to_all x0 -> x1, waiting for transfers between devices: none -> 77 us  [shards(): noise_rows = lax.all_to_all(noise, 'cols', 1, 2, tiled=True)]
    ppermute x0 -> x6, starting transfers between devices: none -> 31.3 us  [the longest x3 28.5 us: line_reduce_scatter(): lax.ppermute(tile(me - count + step) + leftward, axis, left_route)]
    add x0 -> x3, other arithmetic: none -> 14.8 us  [the longest x2 11.9 us: line_reduce_scatter(): tile(me - count + step) + leftward]
    ppermute x3, waiting for transfers between devices: 28.6 us -> 40.8 us  [shifted(): return lax.ppermute(block, axis, route)]
    unnamed x22 -> x27, local copies, waits for them, and re-layouts: 3.39 us -> 11.8 us
    dot_general x20, matrix products: 32.3 us -> 25.2 us  [bdot(): return jnp.dot(left, right, preferred_element_type=jnp.float32)]
  transfers between devices with their start and end apart: 6 -> 11, of which waited for: 5 -> 8; matrix products, arithmetic and copies ran while one was open for 5% -> 7% of each run, Pallas kernels for 0% -> 0%
where the time goes in v5:
time: 434 us; the launch traced here: 429 us
  waiting for transfers between devices  292 us (67%)
  starting transfers between devices  46.6 us (11%)
  other arithmetic  28.9 us (7%)
  matrix products  25.2 us (6%)
  local copies, waits for them, and re-layouts  22.7 us (5%)
  between operations  13.7 us (3%)
    ppermute x3, waiting for transfers between devices, line_reduce_scatter(): lax.ppermute(tile(me - count + step) + leftward, axis, left_route)  135 us
    all_to_all x1, waiting for transfers between devices, shards(): noise_rows = lax.all_to_all(noise, 'cols', 1, 2, tiled=True)  77 us
    ppermute x3, waiting for transfers between devices, shifted(): return lax.ppermute(block, axis, route)  40.8 us
    ppermute x3, waiting for transfers between devices, line_reduce_scatter(): lax.ppermute(tile(me + count - step) + rightward, axis, right_route)  38.8 us
    ppermute x3, starting transfers between devices, line_reduce_scatter(): lax.ppermute(tile(me - count + step) + leftward, axis, left_route)  28.5 us
    dot_general x20, matrix products, bdot(): return jnp.dot(left, right, preferred_element_type=jnp.float32)  25.2 us
    add x2, other arithmetic, line_reduce_scatter(): tile(me - count + step) + leftward  11.9 us
    unnamed x27, local copies, waits for them, and re-layouts  11.8 us
  transfers between devices with their start and end apart: 11, of which 8 were waited for; matrix products, arithmetic and copies ran while one was open for 7% of the time, Pallas kernels for 0%

profile of v5, /device:TPU:25, one launch (start us, length us, event | category | flops | bytes accessed | tf_op | source)
XLA Modules:
  0.0 429.2 jit_solution(12021384803957691349)
XLA Ops:
  6.5 4.5 %copy.12 = f32[2,1024,256]{2,0,1:T(2,128)} copy(f32[2,1024,256]{2,1,0:T(8,128)} %param.6) | data formatting | bytes 4194304 | tf_op args[0]
  11.1 4.5 %all-to-all-start = ((f32[2,1024,256]{2,0,1:T(2,128)}), f32[2,1024,256]{2,0,1:T(2,128)S(1)}, u32[]{:S(2)}, u32[]{:S(2)}) async-start(f32[2,1024,256]{2,0,1:T(2,128)} %copy.12), calls=%async_computation | async-start | bytes 4194304 | tf_op jit(solution)/shard_map/all_to_all | solution.py:62
  16.3 77.0 %all-to-all-done = f32[2,1024,256]{2,0,1:T(2,128)S(1)} async-done(((f32[2,1024,256]{2,0,1:T(2,128)}), f32[2,1024,256]{2,0,1:T(2,128)S(1)}, u32[]{:S(2)}, u32[]{:S(2)}) %all-to-all-start) | async-done | bytes 2097184 | tf_op jit(solution)/shard_map/all_to_all | solution.py:62
  95.1 2.0 copy.17
  104.5 2.6 fusion.32
  108.6 16.4 %collective-permute-start.4 = (f32[2,1024,256]{1,2,0:T(8,128)}, f32[2,1024,256]{1,2,0:T(8,128)}, u32[]{:S(2)}, u32[]{:S(2)}) collective-permute-start(f32[2,1024,256]{1,2,0:T(8,128)} %get-tuple-element.76), channel_id=1, source_target_pairs={{3,2},{7,6},{11,10},{15,14},{19,18},{23,22},{27,26},{31,30}} | collective-permute-start | bytes 6291464 | tf_op jit(solution)/shard_map/ppermute | solution.py:53
  125.0 86.1 %collective-permute-done.4 = f32[2,1024,256]{1,2,0:T(8,128)} collective-permute-done((f32[2,1024,256]{1,2,0:T(8,128)}, f32[2,1024,256]{1,2,0:T(8,128)}, u32[]{:S(2)}, u32[]{:S(2)}) %collective-permute-start.4) | collective-permute-done | bytes 2097184 | tf_op jit(solution)/shard_map/ppermute | solution.py:53
  211.1 6.0 %fusion.43 = (f32[2,1024,256]{1,2,0:T(8,128)}, f32[2,1024,256]{1,2,0:T(8,128)}) fusion(f32[2,1024,256]{1,2,0:T(8,128)} %collective-permute-done.4, s32[]{:T(128)S(6)} %select_n.26, f32[1,1024,1024]{1,2,0:T(8,128)} %copy-done.1, f32[1,1024,1024]{1,2,0:T(8,128)} %copy-done, f32[2,1024,256]{1,2,0:T(8,128)S(1)} %collective-permute-done.1, s32[]{:T(128)S(6)} %select_n.23), kind=kLoop, calls=%fused_computation.75 | loop fusion | flops 2097152 | bytes 16777224 | tf_op jit(solution)/shard_map/add | solution.py:53
  217.8 6.0 %collective-permute-start.5 = (f32[2,1024,256]{1,2,0:T(8,128)}, f32[2,1024,256]{1,2,0:T(8,128)}, u32[]{:S(2)}, u32[]{:S(2)}) collective-permute-start(f32[2,1024,256]{1,2,0:T(8,128)} %get-tuple-element.74), channel_id=1, source_target_pairs={{2,1},{3,2},{6,5},{7,6},{10,9},{11,10},{14,13},{15,14},{18,17},{19... | collective-permute-start | bytes 6291464 | tf_op jit(solution)/shard_map/ppermute | solution.py:53
  223.8 47.6 %collective-permute-done.5 = f32[2,1024,256]{1,2,0:T(8,128)} collective-permute-done((f32[2,1024,256]{1,2,0:T(8,128)}, f32[2,1024,256]{1,2,0:T(8,128)}, u32[]{:S(2)}, u32[]{:S(2)}) %collective-permute-start.5) | collective-permute-done | bytes 2097184 | tf_op jit(solution)/shard_map/ppermute | solution.py:53
  271.4 6.0 %fusion.41 = (f32[2,1024,256]{1,2,0:T(8,128)}, f32[2,1024,256]{1,2,0:T(8,128)}) fusion(f32[2,1024,256]{1,2,0:T(8,128)} %collective-permute-done.5, s32[]{:T(128)S(6)} %select_n.25, f32[1,1024,1024]{1,2,0:T(8,128)} %copy-done.1, f32[1,1024,1024]{1,2,0:T(8,128)} %copy-done, f32[2,1024,256]{1,2,0:T(8,128)S(1)} %collective-permute-done.2, s32[]{:T(128)S(6)} %select_n.22), kind=kLoop, calls=%fused_computation.73 | loop fusion | flops 2097152 | bytes 16777224 | tf_op jit(solution)/shard_map/add | solution.py:53
  278.6 6.1 %collective-permute-start.6 = (f32[2,1024,256]{1,2,0:T(8,128)}, f32[2,1024,256]{1,2,0:T(8,128)}, u32[]{:S(2)}, u32[]{:S(2)}) collective-permute-start(f32[2,1024,256]{1,2,0:T(8,128)} %get-tuple-element.72), channel_id=1, source_target_pairs={{1,0},{2,1},{3,2},{5,4},{6,5},{7,6},{9,8},{10,9},{11,10},{13,12},{... | collective-permute-start | bytes 6291464 | tf_op jit(solution)/shard_map/ppermute | solution.py:53
  284.7 38.8 %collective-permute-done.3 = f32[2,1024,256]{1,2,0:T(8,128)S(1)} collective-permute-done((f32[2,1024,256]{1,2,0:T(8,128)}, f32[2,1024,256]{1,2,0:T(8,128)S(1)}, u32[]{:S(2)}, u32[]{:S(2)}) %collective-permute-start.3) | collective-permute-done | bytes 2097184 | tf_op jit(solution)/shard_map/ppermute | solution.py:52
  324.5 2.9 fusion.34
  328.9 7.3 %fusion.18 = (bf16[1024,1024]{1,0:T(8,128)(2,1)S(1)}, bf16[1024,1024]{1,0:T(8,128)(2,1)}, bf16[1024,1024]{1,0:T(8,128)(2,1)}, bf16[1024,1024]{1,0:T(8,128)(2,1)S(1)}) fusion(f32[2,1024,1024]{2,1,0:T(8,128)} %all-gather.2.cloned.1.call-done), kind=kLoop, calls=%fused_computation.47 | loop fusion | flops 10485760 | bytes 16777216 | tf_op jit(solution)/shard_map/convert_element_type | solution.py:20
  339.4 6.9 %collective-permute-start.7 = (f32[1024,256]{0,1:T(8,128)S(1)}, f32[1024,256]{0,1:T(8,128)S(1)}, u32[]{:S(2)}, u32[]{:S(2)}) collective-permute-start(f32[1024,256]{0,1:T(8,128)S(1)} %fusion.66), channel_id=1, source_target_pairs={{4,0},{8,4},{12,8},{5,1},{9,5},{13,9},{6,2},{10,6},{14,10},{7,3},{... | collective-permute-start | bytes 3145736 | tf_op jit(solution)/shard_map/ppermute | solution.py:12
  347.8 12.1 %collective-permute-done.7 = f32[1024,256]{0,1:T(8,128)S(1)} collective-permute-done((f32[1024,256]{0,1:T(8,128)S(1)}, f32[1024,256]{0,1:T(8,128)S(1)}, u32[]{:S(2)}, u32[]{:S(2)}) %collective-permute-start.7) | collective-permute-done | bytes 1048608 | tf_op jit(solution)/shard_map/ppermute | solution.py:12
  359.9 48.9 %while.10 = (s32[]{:T(128)}, f32[1024,256]{0,1:T(8,128)S(1)}, bf16[1024,1024]{1,0:T(8,128)(2,1)}, bf16[1024,1024]{1,0:T(8,128)(2,1)}, f32[1024,256]{0,1:T(8,128)...) while((s32[]{:T(128)}, f32[1024,256]{0,1:T(8,128)S(1)}, ...), condition=%wide.region_1.2_spmd, body=%wide.region_0.1_spmd.sunk | while | flops 3229614080 | bytes 63963408 | solution.py:86
  368.0 1.9 collective-permute-start
  369.9 14.4 %collective-permute-done = f32[1024,256]{0,1:T(8,128)S(1)} collective-permute-done((f32[1024,256]{0,1:T(8,128)}, f32[1024,256]{0,1:T(8,128)S(1)}, u32[]{:S(2)}, u32[]{:S(2)}) %collective-permute-start) | collective-permute-done | bytes 1048608 | tf_op jit(solution)/shard_map/while/body/eval_jaxpr/ppermute | solution.py:12
  392.4 1.9 collective-permute-start
  394.4 14.4 %collective-permute-done = f32[1024,256]{0,1:T(8,128)S(1)} collective-permute-done((f32[1024,256]{0,1:T(8,128)}, f32[1024,256]{0,1:T(8,128)S(1)}, u32[]{:S(2)}, u32[]{:S(2)}) %collective-permute-start) | collective-permute-done | bytes 1048608 | tf_op jit(solution)/shard_map/while/body/eval_jaxpr/ppermute | solution.py:12
  416.5 2.0 fusion.27
  418.4 2.0 fusion.28
  (87 shorter events, 46.2 us)
Async XLA Ops:
  11.1 82.2 %all-to-all-start = ((f32[2,1024,256]{2,0,1:T(2,128)}), f32[2,1024,256]{2,0,1:T(2,128)S(1)}, u32[]{:S(2)}, u32[]{:S(2)}) async-start(f32[2,1024,256]{2,0,1:T(2,128)} %copy.12), calls=%async_computation | async-start | bytes 4194304 | tf_op jit(solution)/shard_map/all_to_all | solution.py:62
  15.6 313.3 %all-gather.2.cloned.1.call-start = ((), (), s32[]{:S(2)}) async-start(), calls=%async_computation.1 | async-start | bytes 10485760 | tf_op jit(solution)/shard_map/all_gather | solution.py:61
  98.7 1.6 copy-start.9
  102.4 2.1 copy-start
  104.5 3.3 copy-start.1
  107.8 17.2 %collective-permute-start.1 = (f32[2,1024,256]{1,2,0:T(8,128)}, f32[2,1024,256]{1,2,0:T(8,128)S(1)}, u32[]{:S(2)}, u32[]{:S(2)}) collective-permute-start(f32[2,1024,256]{1,2,0:T(8,128)} %get-tuple-element.77), channel_id=1, source_target_pairs={{0,1},{4,5},{8,9},{12,13},{16,17},{20,21},{24,25},{28,29}} | collective-permute-start | bytes 6291464 | tf_op jit(solution)/shard_map/ppermute | solution.py:52
  108.6 102.5 %collective-permute-start.4 = (f32[2,1024,256]{1,2,0:T(8,128)}, f32[2,1024,256]{1,2,0:T(8,128)}, u32[]{:S(2)}, u32[]{:S(2)}) collective-permute-start(f32[2,1024,256]{1,2,0:T(8,128)} %get-tuple-element.76), channel_id=1, source_target_pairs={{3,2},{7,6},{11,10},{15,14},{19,18},{23,22},{27,26},{31,30}} | collective-permute-start | bytes 6291464 | tf_op jit(solution)/shard_map/ppermute | solution.py:53
  217.0 6.8 %collective-permute-start.2 = (f32[2,1024,256]{1,2,0:T(8,128)}, f32[2,1024,256]{1,2,0:T(8,128)S(1)}, u32[]{:S(2)}, u32[]{:S(2)}) collective-permute-start(f32[2,1024,256]{1,2,0:T(8,128)} %get-tuple-element.75), channel_id=1, source_target_pairs={{0,1},{1,2},{4,5},{5,6},{8,9},{9,10},{12,13},{13,14},{16,17},{17,1... | collective-permute-start | bytes 6291464 | tf_op jit(solution)/shard_map/ppermute | solution.py:52
  217.8 53.5 %collective-permute-start.5 = (f32[2,1024,256]{1,2,0:T(8,128)}, f32[2,1024,256]{1,2,0:T(8,128)}, u32[]{:S(2)}, u32[]{:S(2)}) collective-permute-start(f32[2,1024,256]{1,2,0:T(8,128)} %get-tuple-element.74), channel_id=1, source_target_pairs={{2,1},{3,2},{6,5},{7,6},{10,9},{11,10},{14,13},{15,14},{18,17},{19... | collective-permute-start | bytes 6291464 | tf_op jit(solution)/shard_map/ppermute | solution.py:53
  277.3 46.1 %collective-permute-start.3 = (f32[2,1024,256]{1,2,0:T(8,128)}, f32[2,1024,256]{1,2,0:T(8,128)S(1)}, u32[]{:S(2)}, u32[]{:S(2)}) collective-permute-start(f32[2,1024,256]{1,2,0:T(8,128)} %get-tuple-element.73), channel_id=1, source_target_pairs={{0,1},{1,2},{2,3},{4,5},{5,6},{6,7},{8,9},{9,10},{10,11},{12,13},{... | collective-permute-start | bytes 6291464 | tf_op jit(solution)/shard_map/ppermute | solution.py:52
  278.6 45.8 %collective-permute-start.6 = (f32[2,1024,256]{1,2,0:T(8,128)}, f32[2,1024,256]{1,2,0:T(8,128)}, u32[]{:S(2)}, u32[]{:S(2)}) collective-permute-start(f32[2,1024,256]{1,2,0:T(8,128)} %get-tuple-element.72), channel_id=1, source_target_pairs={{1,0},{2,1},{3,2},{5,4},{6,5},{7,6},{9,8},{10,9},{11,10},{13,12},{... | collective-permute-start | bytes 6291464 | tf_op jit(solution)/shard_map/ppermute | solution.py:53
  328.9 8.7 %copy-start.10 = (f32[2,1024,1024]{2,1,0:T(8,128)S(1)}, f32[2,1024,1024]{2,1,0:T(8,128)}, u32[]{:S(2)}) copy-start(f32[2,1024,1024]{2,1,0:T(8,128)} %all-gather.2.cloned.1.call-done) | copy-start | bytes 25165828
  336.2 2.3 copy-start.7
  339.4 20.5 %collective-permute-start.7 = (f32[1024,256]{0,1:T(8,128)S(1)}, f32[1024,256]{0,1:T(8,128)S(1)}, u32[]{:S(2)}, u32[]{:S(2)}) collective-permute-start(f32[1024,256]{0,1:T(8,128)S(1)} %fusion.66), channel_id=1, source_target_pairs={{4,0},{8,4},{12,8},{5,1},{9,5},{13,9},{6,2},{10,6},{14,10},{7,3},{... | collective-permute-start | bytes 3145736 | tf_op jit(solution)/shard_map/ppermute | solution.py:12
  359.9 1.6 copy-start.15
  361.5 1.6 copy-start.2
  361.5 1.9 copy-start.5
  368.0 16.3 %collective-permute-start = (f32[1024,256]{0,1:T(8,128)}, f32[1024,256]{0,1:T(8,128)S(1)}, u32[]{:S(2)}, u32[]{:S(2)}) collective-permute-start(f32[1024,256]{0,1:T(8,128)} %fusion.157), channel_id=1, source_target_pairs={{4,0},{8,4},{12,8},{5,1},{9,5},{13,9},{6,2},{10,6},{14,10},{7,3},{... | collective-permute-start | bytes 3145736 | tf_op jit(solution)/shard_map/while/body/eval_jaxpr/ppermute | solution.py:12
  384.3 1.6 copy-start.15
  385.9 1.6 copy-start.2
  385.9 1.9 copy-start.5
  392.4 16.3 %collective-permute-start = (f32[1024,256]{0,1:T(8,128)}, f32[1024,256]{0,1:T(8,128)S(1)}, u32[]{:S(2)}, u32[]{:S(2)}) collective-permute-start(f32[1024,256]{0,1:T(8,128)} %fusion.157), channel_id=1, source_target_pairs={{4,0},{8,4},{12,8},{5,1},{9,5},{13,9},{6,2},{10,6},{14,10},{7,3},{... | collective-permute-start | bytes 3145736 | tf_op jit(solution)/shard_map/while/body/eval_jaxpr/ppermute | solution.py:12
  408.8 1.6 copy-start.16
  410.4 2.2 copy-start.8
  (10 other events, 14.0 us)
Sparse Core Ops, SparseCore 0:
  18.0 215.5 all-gather.1

commit v6 on v5

--- a/solution.py
+++ b/solution.py
@@ -54,12 +54,53 @@
     return tile(me) + (rightward + leftward)
 
 
+def add_at(whole, piece, slot, axis):
+    count = whole.shape[axis] // piece.shape[axis]
+    start = jnp.clip(slot, 0, count - 1) * piece.shape[axis]
+    current = lax.dynamic_slice_in_dim(whole, start, piece.shape[axis], axis=axis)
+    return lax.dynamic_update_slice_in_dim(whole, current + piece, start, axis=axis)
+
+
+def line_all_gather(tile, axis):
+    count = lax.axis_size(axis)
+    me = lax.axis_index(axis)
+    last = tile.ndim - 1
+    shape = tile.shape[:-1] + (count * tile.shape[-1],)
+    whole = add_at(jnp.zeros(shape, tile.dtype), tile, me, last)
+    from_left = tile
+    from_right = tile
+    for step in range(1, count):
+        from_left = lax.ppermute(from_left, axis, [(k, k + 1) for k in range(step - 1, count - 1)])
+        from_right = lax.ppermute(from_right, axis, [(k, k - 1) for k in range(1, count - step + 1)])
+        whole = add_at(whole, from_left, me - step, last)
+        whole = add_at(whole, from_right, me + step, last)
+    return whole
+
+
+def line_all_to_all(value, axis):
+    count = lax.axis_size(axis)
+    me = lax.axis_index(axis)
+    rows = value.shape[1] // count
+
+    def own_rows(target):
+        return lax.dynamic_slice_in_dim(value, jnp.clip(target, 0, count - 1) * rows, rows, axis=1)
+
+    shape = (value.shape[0], rows, count * value.shape[2])
+    whole = add_at(jnp.zeros(shape, value.dtype), own_rows(me), me, 2)
+    for distance in range(1, count):
+        right = lax.ppermute(own_rows(me + distance), axis, [(k, k + distance) for k in range(0, count - distance)])
+        left = lax.ppermute(own_rows(me - distance), axis, [(k, k - distance) for k in range(distance, count)])
+        whole = add_at(whole, right, me - distance, 2)
+        whole = add_at(whole, left, me + distance, 2)
+    return whole
+
+
 def shards(noise, inv_diag, coupling, order):
     block_count = noise.shape[0]
     node_count = noise.shape[1]
     sample_count = noise.shape[2]
-    coupling_full = lax.all_gather(coupling, "cols", axis=2, tiled=True)
-    noise_rows = lax.all_to_all(noise, "cols", 1, 2, tiled=True)
+    coupling_full = line_all_gather(coupling, "cols")
+    noise_rows = line_all_to_all(noise, "cols")
     partial = jnp.stack(
         [apply(split(inv_diag[block], 2), noise_rows[block]) for block in range(block_count)], axis=0
     )

time: 434 us -> 340 us (0.78)
  waiting for transfers between devices: 292 us -> 217 us
  between operations: 13.7 us -> 0.52 us
  local copies, waits for them, and re-layouts: 22.7 us -> 14.5 us
  starting transfers between devices: 46.6 us -> 54.7 us
    all_to_all x1 -> x0, waiting for transfers between devices: 77 us -> none  [shards(): noise_rows = lax.all_to_all(noise, 'cols', 1, 2, tiled=True)]
    ppermute x0 -> x12, waiting for transfers between devices: none -> 61.5 us  [the longest x3 29.8 us: line_all_to_all(): lax.ppermute(own_rows(me + distance), axis, [(k, k + distance) for k in r...]
    ppermute x3, waiting for transfers between devices: 38.8 us -> 5.23 us  [line_reduce_scatter(): lax.ppermute(tile(me + count - step) + rightward, axis, right_route)]
    ppermute x3, waiting for transfers between devices: 135 us -> 109 us  [line_reduce_scatter(): lax.ppermute(tile(me - count + step) + leftward, axis, left_route)]
    ppermute x0 -> x12, starting transfers between devices: none -> 24.1 us  [the longest x3 13 us: line_all_to_all(): lax.ppermute(own_rows(me - distance), axis, [(k, k - distance) for k in r...]
    ppermute x3, starting transfers between devices: 28.5 us -> 15 us  [line_reduce_scatter(): lax.ppermute(tile(me - count + step) + leftward, axis, left_route)]
    dynamic_update_slice x0 -> x12, other arithmetic: none -> 4.56 us  [add_at(): lax.dynamic_update_slice_in_dim(whole, current + piece, start, axis=axis)]
    all_to_all x1 -> x0, starting transfers between devices: 4.53 us -> none  [shards(): noise_rows = lax.all_to_all(noise, 'cols', 1, 2, tiled=True)]
  transfers between devices with their start and end apart: 11 -> 21, of which waited for: 8 -> 11; matrix products, arithmetic and copies ran while one was open for 7% -> 7% of each run, Pallas kernels for 0% -> 0%
where the time goes in v6:
time: 340 us; the launch traced here: 339 us
  waiting for transfers between devices  217 us (64%)
  starting transfers between devices  54.7 us (16%)
  other arithmetic  27.8 us (8%)
  matrix products  25 us (7%)
  local copies, waits for them, and re-layouts  14.5 us (4%)
    ppermute x3, waiting for transfers between devices, line_reduce_scatter(): lax.ppermute(tile(me - count + step) + leftward, axis, left_route)  109 us
    ppermute x3, waiting for transfers between devices, shifted(): return lax.ppermute(block, axis, route)  40.9 us
    ppermute x3, waiting for transfers between devices, line_all_to_all(): lax.ppermute(own_rows(me + distance), axis, [(k, k + distance) for k in r...  29.8 us
    ppermute x3, waiting for transfers between devices, line_all_gather(): lax.ppermute(from_left, axis, [(k, k + 1) for k in range(step - 1, count...  27.2 us
    dot_general x20, matrix products, bdot(): return jnp.dot(left, right, preferred_element_type=jnp.float32)  25 us
    ppermute x3, starting transfers between devices, line_reduce_scatter(): lax.ppermute(tile(me - count + step) + leftward, axis, left_route)  15 us
    ppermute x3, starting transfers between devices, line_all_to_all(): lax.ppermute(own_rows(me - distance), axis, [(k, k - distance) for k in r...  13 us
    ppermute x3, starting transfers between devices, shifted(): return lax.ppermute(block, axis, route)  11.4 us
  transfers between devices with their start and end apart: 21, of which 11 were waited for; matrix products, arithmetic and copies ran while one was open for 7% of the time, Pallas kernels for 0%

profile of v6, /device:TPU:25, one launch (start us, length us, event | category | flops | bytes accessed | tf_op | source)
XLA Modules:
  0.0 339.2 jit_solution(4304777126216204170)
XLA Ops:
  3.4 4.0 %collective-permute-start.2 = (f32[2,256,256]{2,1,0:T(8,128)S(1)}, f32[2,256,256]{2,1,0:T(8,128)S(1)}, u32[]{:S(2)}, u32[]{:S(2)}) collective-permute-start(f32[2,256,256]{2,1,0:T(8,128)S(1)} %get-tuple-element.93), channel_id=1, source_target_pairs={{1,0},{2,1},{3,2},{5,4},{6,5},{7,6},{9,8},{10,9},{11,10},{13,12},{... | collective-permute-start | bytes 1572872 | tf_op jit(solution)/shard_map/ppermute | solution.py:92
  8.7 4.9 %collective-permute-start.4 = (f32[2,256,256]{2,1,0:T(8,128)S(1)}, f32[2,256,256]{2,1,0:T(8,128)S(1)}, u32[]{:S(2)}, u32[]{:S(2)}) collective-permute-start(f32[2,256,256]{2,1,0:T(8,128)S(1)} %get-tuple-element.91), channel_id=1, source_target_pairs={{2,0},{3,1},{6,4},{7,5},{10,8},{11,9},{14,12},{15,13},{18,16},{19,... | collective-permute-start | bytes 1572872 | tf_op jit(solution)/shard_map/ppermute | solution.py:92
  16.9 4.1 %collective-permute-start.6 = (f32[2,256,256]{2,1,0:T(8,128)S(1)}, f32[2,256,256]{2,1,0:T(8,128)S(1)}, u32[]{:S(2)}, u32[]{:S(2)}) collective-permute-start(f32[2,256,256]{2,1,0:T(8,128)S(1)} %get-tuple-element.90), channel_id=1, source_target_pairs={{3,0},{7,4},{11,8},{15,12},{19,16},{23,20},{27,24},{31,28}} | collective-permute-start | bytes 1572872 | tf_op jit(solution)/shard_map/ppermute | solution.py:92
  22.4 28.0 %collective-permute-done.3 = f32[2,256,256]{2,1,0:T(8,128)S(1)} collective-permute-done((f32[2,256,256]{2,1,0:T(8,128)S(1)}, f32[2,256,256]{2,1,0:T(8,128)S(1)}, u32[]{:S(2)}, u32[]{:S(2)}) %collective-permute-start.3) | collective-permute-done | bytes 524320 | tf_op jit(solution)/shard_map/ppermute | solution.py:91
  58.5 2.0 collective-permute-start.10
  61.3 27.2 %collective-permute-done.13 = f32[2,1024,256]{2,1,0:T(8,128)S(1)} collective-permute-done((f32[2,1024,256]{2,1,0:T(8,128)S(1)}, f32[2,1024,256]{2,1,0:T(8,128)S(1)}, u32[]{:S(2)}, u32[]{:S(2)}) %collective-permute-start.13) | collective-permute-done | bytes 2097184 | tf_op jit(solution)/shard_map/ppermute | solution.py:73
  89.8 4.5 %collective-permute-done.14 = f32[2,1024,256]{2,1,0:T(8,128)S(1)} collective-permute-done((f32[2,1024,256]{2,1,0:T(8,128)S(1)}, f32[2,1024,256]{2,1,0:T(8,128)S(1)}, u32[]{:S(2)}, u32[]{:S(2)}) %collective-permute-start.14) | collective-permute-done | bytes 2097184 | tf_op jit(solution)/shard_map/ppermute | solution.py:74
  95.1 44.1 %collective-permute-done.10 = f32[2,1024,256]{1,2,0:T(8,128)S(1)} collective-permute-done((f32[2,1024,256]{1,2,0:T(8,128)S(1)}, f32[2,1024,256]{1,2,0:T(8,128)S(1)}, u32[]{:S(2)}, u32[]{:S(2)}) %collective-permute-start.10) | collective-permute-done | bytes 2097184 | tf_op jit(solution)/shard_map/ppermute | solution.py:53
  139.2 3.0 fusion.43
  142.2 5.4 %collective-permute-start.11 = (f32[2,1024,256]{1,2,0:T(8,128)}, f32[2,1024,256]{1,2,0:T(8,128)}, u32[]{:S(2)}, u32[]{:S(2)}) collective-permute-start(f32[2,1024,256]{1,2,0:T(8,128)} %get-tuple-element.78), channel_id=1, source_target_pairs={{2,1},{3,2},{6,5},{7,6},{10,9},{11,10},{14,13},{15,14},{18,17},{19... | collective-permute-start | bytes 6291464 | tf_op jit(solution)/shard_map/ppermute | solution.py:53
  147.7 2.1 collective-permute-start.8
  154.2 34.0 %collective-permute-done.11 = f32[2,1024,256]{1,2,0:T(8,128)} collective-permute-done((f32[2,1024,256]{1,2,0:T(8,128)}, f32[2,1024,256]{1,2,0:T(8,128)}, u32[]{:S(2)}, u32[]{:S(2)}) %collective-permute-start.11) | collective-permute-done | bytes 2097184 | tf_op jit(solution)/shard_map/ppermute | solution.py:53
  188.2 5.2 %fusion.41 = (f32[2,1024,256]{1,2,0:T(8,128)}, f32[2,1024,256]{1,2,0:T(8,128)}) fusion(f32[2,1024,256]{1,2,0:T(8,128)} %collective-permute-done.11, s32[]{:T(128)S(6)} %select_n.15, f32[1,1024,1024]{1,2,0:T(8,128)S(1)} %fusion.26, f32[1,1024,1024]{1,2,0:T(8,128)S(1)} %fusion.24, f32[2,1024,256]{1,2,0:T(8,128)} %collective-permute-done.8, s32[]{:T(128)S(6)} %select_n.16), kind=kLoop, calls=%fused_computation.73 | loop fusion | flops 2097152 | bytes 16777224 | tf_op jit(solution)/shard_map/add | solution.py:53
  193.4 7.6 %collective-permute-start.12 = (f32[2,1024,256]{1,2,0:T(8,128)}, f32[2,1024,256]{1,2,0:T(8,128)}, u32[]{:S(2)}, u32[]{:S(2)}) collective-permute-start(f32[2,1024,256]{1,2,0:T(8,128)} %get-tuple-element.76), channel_id=1, source_target_pairs={{1,0},{2,1},{3,2},{5,4},{6,5},{7,6},{9,8},{10,9},{11,10},{13,12},{... | collective-permute-start | bytes 6291464 | tf_op jit(solution)/shard_map/ppermute | solution.py:53
  205.4 4.3 %fusion.18 = (bf16[1024,1024]{1,0:T(8,128)(2,1)S(1)}, bf16[1024,1024]{1,0:T(8,128)(2,1)}, bf16[1024,1024]{1,0:T(8,128)(2,1)}, bf16[1024,1024]{1,0:T(8,128)(2,1)}) fusion(f32[2,1024,1024]{2,1,0:T(8,128)S(1)} %add_dynamic-update-slice_fusion), kind=kLoop, calls=%fused_computation.47 | loop fusion | flops 10485760 | bytes 16777216 | tf_op jit(solution)/shard_map/convert_element_type | solution.py:20
  209.7 30.8 %collective-permute-done.12 = f32[2,1024,256]{1,2,0:T(8,128)} collective-permute-done((f32[2,1024,256]{1,2,0:T(8,128)}, f32[2,1024,256]{1,2,0:T(8,128)}, u32[]{:S(2)}, u32[]{:S(2)}) %collective-permute-start.12) | collective-permute-done | bytes 2097184 | tf_op jit(solution)/shard_map/ppermute | solution.py:53
  240.5 5.2 %collective-permute-done.9 = f32[2,1024,256]{1,2,0:T(8,128)} collective-permute-done((f32[2,1024,256]{1,2,0:T(8,128)}, f32[2,1024,256]{1,2,0:T(8,128)}, u32[]{:S(2)}, u32[]{:S(2)}) %collective-permute-start.9) | collective-permute-done | bytes 2097184 | tf_op jit(solution)/shard_map/ppermute | solution.py:52
  245.8 2.9 fusion.34
  248.9 2.1 copy-done.10
  253.2 7.6 %collective-permute-start.19 = (f32[1024,256]{0,1:T(8,128)S(1)}, f32[1024,256]{0,1:T(8,128)}, u32[]{:S(2)}, u32[]{:S(2)}) collective-permute-start(f32[1024,256]{0,1:T(8,128)S(1)} %fusion.81), channel_id=1, source_target_pairs={{4,0},{8,4},{12,8},{5,1},{9,5},{13,9},{6,2},{10,6},{14,10},{7,3},{... | collective-permute-start | bytes 3145736 | tf_op jit(solution)/shard_map/ppermute | solution.py:12
  262.3 11.9 %collective-permute-done.19 = f32[1024,256]{0,1:T(8,128)} collective-permute-done((f32[1024,256]{0,1:T(8,128)S(1)}, f32[1024,256]{0,1:T(8,128)}, u32[]{:S(2)}, u32[]{:S(2)}) %collective-permute-start.19) | collective-permute-done | bytes 1048608 | tf_op jit(solution)/shard_map/ppermute | solution.py:12
  274.2 49.7 %while.10 = (s32[]{:T(128)}, f32[1024,256]{0,1:T(8,128)}, bf16[1024,1024]{1,0:T(8,128)(2,1)}, bf16[1024,1024]{1,0:T(8,128)(2,1)}, f32[1024,256]{0,1:T(8,128)}, /...) while((s32[]{:T(128)}, f32[1024,256]{0,1:T(8,128)}, ...), condition=%wide.region_1.2_spmd, body=%wide.region_0.1_spmd.sunk | while | flops 3229614080 | bytes 63963408 | solution.py:127
  284.6 14.5 %collective-permute-done = f32[1024,256]{0,1:T(8,128)} collective-permute-done((f32[1024,256]{0,1:T(8,128)}, f32[1024,256]{0,1:T(8,128)}, u32[]{:S(2)}, u32[]{:S(2)}) %collective-permute-start) | collective-permute-done | bytes 1048608 | tf_op jit(solution)/shard_map/while/body/eval_jaxpr/ppermute | solution.py:12
  309.4 14.5 %collective-permute-done = f32[1024,256]{0,1:T(8,128)} collective-permute-done((f32[1024,256]{0,1:T(8,128)}, f32[1024,256]{0,1:T(8,128)}, u32[]{:S(2)}, u32[]{:S(2)}) %collective-permute-start) | collective-permute-done | bytes 1048608 | tf_op jit(solution)/shard_map/while/body/eval_jaxpr/ppermute | solution.py:12
  (112 shorter events, 68.5 us)
Async XLA Ops:
  1.9 19.2 %copy-start.8 = (f32[2,1024,256]{2,1,0:T(8,128)S(1)}, f32[2,1024,256]{2,1,0:T(8,128)}, u32[]{:S(2)}) copy-start(f32[2,1024,256]{2,1,0:T(8,128)} %param.8) | copy-start | bytes 6291460
  1.9 14.8 %collective-permute-start.1 = (f32[2,256,256]{2,1,0:T(8,128)S(1)}, f32[2,256,256]{2,1,0:T(8,128)S(1)}, u32[]{:S(2)}, u32[]{:S(2)}) collective-permute-start(f32[2,256,256]{2,1,0:T(8,128)S(1)} %get-tuple-element.94), channel_id=1, source_target_pairs={{0,1},{1,2},{2,3},{4,5},{5,6},{6,7},{8,9},{9,10},{10,11},{12,13},{... | collective-permute-start | bytes 1572872 | tf_op jit(solution)/shard_map/ppermute | solution.py:91
  3.4 17.6 %collective-permute-start.2 = (f32[2,256,256]{2,1,0:T(8,128)S(1)}, f32[2,256,256]{2,1,0:T(8,128)S(1)}, u32[]{:S(2)}, u32[]{:S(2)}) collective-permute-start(f32[2,256,256]{2,1,0:T(8,128)S(1)} %get-tuple-element.93), channel_id=1, source_target_pairs={{1,0},{2,1},{3,2},{5,4},{6,5},{7,6},{9,8},{10,9},{11,10},{13,12},{... | collective-permute-start | bytes 1572872 | tf_op jit(solution)/shard_map/ppermute | solution.py:92
  7.4 43.0 %collective-permute-start.3 = (f32[2,256,256]{2,1,0:T(8,128)S(1)}, f32[2,256,256]{2,1,0:T(8,128)S(1)}, u32[]{:S(2)}, u32[]{:S(2)}) collective-permute-start(f32[2,256,256]{2,1,0:T(8,128)S(1)} %get-tuple-element.92), channel_id=1, source_target_pairs={{0,2},{1,3},{4,6},{5,7},{8,10},{9,11},{12,14},{13,15},{16,18},{17,... | collective-permute-start | bytes 1572872 | tf_op jit(solution)/shard_map/ppermute | solution.py:91
  8.7 43.3 %collective-permute-start.4 = (f32[2,256,256]{2,1,0:T(8,128)S(1)}, f32[2,256,256]{2,1,0:T(8,128)S(1)}, u32[]{:S(2)}, u32[]{:S(2)}) collective-permute-start(f32[2,256,256]{2,1,0:T(8,128)S(1)} %get-tuple-element.91), channel_id=1, source_target_pairs={{2,0},{3,1},{6,4},{7,5},{10,8},{11,9},{14,12},{15,13},{18,16},{19,... | collective-permute-start | bytes 1572872 | tf_op jit(solution)/shard_map/ppermute | solution.py:92
  13.6 38.5 %collective-permute-start.5 = (f32[2,256,256]{2,1,0:T(8,128)S(1)}, f32[2,256,256]{2,1,0:T(8,128)S(1)}, u32[]{:S(2)}, u32[]{:S(2)}) collective-permute-start(f32[2,256,256]{2,1,0:T(8,128)S(1)} %get-tuple-element.96), channel_id=1, source_target_pairs={{0,3},{4,7},{8,11},{12,15},{16,19},{20,23},{24,27},{28,31}} | collective-permute-start | bytes 1572872 | tf_op jit(solution)/shard_map/ppermute | solution.py:91
  16.9 35.4 %collective-permute-start.6 = (f32[2,256,256]{2,1,0:T(8,128)S(1)}, f32[2,256,256]{2,1,0:T(8,128)S(1)}, u32[]{:S(2)}, u32[]{:S(2)}) collective-permute-start(f32[2,256,256]{2,1,0:T(8,128)S(1)} %get-tuple-element.90), channel_id=1, source_target_pairs={{3,0},{7,4},{11,8},{15,12},{19,16},{23,20},{27,24},{31,28}} | collective-permute-start | bytes 1572872 | tf_op jit(solution)/shard_map/ppermute | solution.py:92
  21.1 67.4 %collective-permute-start.13 = (f32[2,1024,256]{2,1,0:T(8,128)S(1)}, f32[2,1024,256]{2,1,0:T(8,128)S(1)}, u32[]{:S(2)}, u32[]{:S(2)}) collective-permute-start(f32[2,1024,256]{2,1,0:T(8,128)S(1)} %copy-done.8), channel_id=1, source_target_pairs={{0,1},{1,2},{2,3},{4,5},{5,6},{6,7},{8,9},{9,10},{10,11},{12,13},{... | collective-permute-start | bytes 6291464 | tf_op jit(solution)/shard_map/ppermute | solution.py:73
  50.5 43.8 %collective-permute-start.14 = (f32[2,1024,256]{2,1,0:T(8,128)S(1)}, f32[2,1024,256]{2,1,0:T(8,128)S(1)}, u32[]{:S(2)}, u32[]{:S(2)}) collective-permute-start(f32[2,1024,256]{2,1,0:T(8,128)S(1)} %copy-done.8), channel_id=1, source_target_pairs={{1,0},{2,1},{3,2},{5,4},{6,5},{7,6},{9,8},{10,9},{11,10},{13,12},{... | collective-permute-start | bytes 6291464 | tf_op jit(solution)/shard_map/ppermute | solution.py:74
  58.5 80.7 %collective-permute-start.10 = (f32[2,1024,256]{1,2,0:T(8,128)S(1)}, f32[2,1024,256]{1,2,0:T(8,128)S(1)}, u32[]{:S(2)}, u32[]{:S(2)}) collective-permute-start(f32[2,1024,256]{1,2,0:T(8,128)S(1)} %get-tuple-element.80), channel_id=1, source_target_pairs={{3,2},{7,6},{11,10},{15,14},{19,18},{23,22},{27,26},{31,30}} | collective-permute-start | bytes 6291464 | tf_op jit(solution)/shard_map/ppermute | solution.py:53
  60.5 78.7 %collective-permute-start.7 = (f32[2,1024,256]{1,2,0:T(8,128)S(1)}, f32[2,1024,256]{1,2,0:T(8,128)S(1)}, u32[]{:S(2)}, u32[]{:S(2)}) collective-permute-start(f32[2,1024,256]{1,2,0:T(8,128)S(1)} %get-tuple-element.81), channel_id=1, source_target_pairs={{0,1},{4,5},{8,9},{12,13},{16,17},{20,21},{24,25},{28,29}} | collective-permute-start | bytes 6291464 | tf_op jit(solution)/shard_map/ppermute | solution.py:52
  88.5 61.3 %collective-permute-start.15 = (f32[2,1024,256]{2,1,0:T(8,128)S(1)}, f32[2,1024,256]{2,1,0:T(8,128)S(1)}, u32[]{:S(2)}, u32[]{:S(2)}) collective-permute-start(f32[2,1024,256]{2,1,0:T(8,128)S(1)} %collective-permute-done.13), channel_id=1, source_target_pairs={{1,2},{2,3},{5,6},{6,7},{9,10},{10,11},{13,14},{14,15},{17,18},{18... | collective-permute-start | bytes 6291464 | tf_op jit(solution)/shard_map/ppermute | solution.py:73
  94.3 56.8 %collective-permute-start.16 = (f32[2,1024,256]{2,1,0:T(8,128)S(1)}, f32[2,1024,256]{2,1,0:T(8,128)S(1)}, u32[]{:S(2)}, u32[]{:S(2)}) collective-permute-start(f32[2,1024,256]{2,1,0:T(8,128)S(1)} %collective-permute-done.14), channel_id=1, source_target_pairs={{1,0},{2,1},{5,4},{6,5},{9,8},{10,9},{13,12},{14,13},{17,16},{18,1... | collective-permute-start | bytes 6291464 | tf_op jit(solution)/shard_map/ppermute | solution.py:74
  142.2 46.0 %collective-permute-start.11 = (f32[2,1024,256]{1,2,0:T(8,128)}, f32[2,1024,256]{1,2,0:T(8,128)}, u32[]{:S(2)}, u32[]{:S(2)}) collective-permute-start(f32[2,1024,256]{1,2,0:T(8,128)} %get-tuple-element.78), channel_id=1, source_target_pairs={{2,1},{3,2},{6,5},{7,6},{10,9},{11,10},{14,13},{15,14},{18,17},{19... | collective-permute-start | bytes 6291464 | tf_op jit(solution)/shard_map/ppermute | solution.py:53
  147.7 5.5 %copy-start.9 = (f32[2,1024,256]{2,1,0:T(8,128)S(1)}, f32[2,1024,256]{2,1,0:T(8,128)}, u32[]{:S(2)}) copy-start(f32[2,1024,256]{2,1,0:T(8,128)} %param.8) | copy-start | bytes 6291460
  147.7 40.5 %collective-permute-start.8 = (f32[2,1024,256]{1,2,0:T(8,128)}, f32[2,1024,256]{1,2,0:T(8,128)}, u32[]{:S(2)}, u32[]{:S(2)}) collective-permute-start(f32[2,1024,256]{1,2,0:T(8,128)} %get-tuple-element.79), channel_id=1, source_target_pairs={{0,1},{1,2},{4,5},{5,6},{8,9},{9,10},{12,13},{13,14},{16,17},{17,1... | collective-permute-start | bytes 6291464 | tf_op jit(solution)/shard_map/ppermute | solution.py:52
  149.8 54.3 %collective-permute-start.17 = (f32[2,1024,256]{2,1,0:T(8,128)S(1)}, f32[2,1024,256]{2,1,0:T(8,128)S(1)}, u32[]{:S(2)}, u32[]{:S(2)}) collective-permute-start(f32[2,1024,256]{2,1,0:T(8,128)S(1)} %collective-permute-done.15), channel_id=1, source_target_pairs={{2,3},{6,7},{10,11},{14,15},{18,19},{22,23},{26,27},{30,31}} | collective-permute-start | bytes 6291464 | tf_op jit(solution)/shard_map/ppermute | solution.py:73
  151.1 53.6 %collective-permute-start.18 = (f32[2,1024,256]{2,1,0:T(8,128)S(1)}, f32[2,1024,256]{2,1,0:T(8,128)S(1)}, u32[]{:S(2)}, u32[]{:S(2)}) collective-permute-start(f32[2,1024,256]{2,1,0:T(8,128)S(1)} %collective-permute-done.16), channel_id=1, source_target_pairs={{1,0},{5,4},{9,8},{13,12},{17,16},{21,20},{25,24},{29,28}} | collective-permute-start | bytes 6291464 | tf_op jit(solution)/shard_map/ppermute | solution.py:74
  193.4 47.1 %collective-permute-start.12 = (f32[2,1024,256]{1,2,0:T(8,128)}, f32[2,1024,256]{1,2,0:T(8,128)}, u32[]{:S(2)}, u32[]{:S(2)}) collective-permute-start(f32[2,1024,256]{1,2,0:T(8,128)} %get-tuple-element.76), channel_id=1, source_target_pairs={{1,0},{2,1},{3,2},{5,4},{6,5},{7,6},{9,8},{10,9},{11,10},{13,12},{... | collective-permute-start | bytes 6291464 | tf_op jit(solution)/shard_map/ppermute | solution.py:53
  201.0 44.8 %collective-permute-start.9 = (f32[2,1024,256]{1,2,0:T(8,128)}, f32[2,1024,256]{1,2,0:T(8,128)}, u32[]{:S(2)}, u32[]{:S(2)}) collective-permute-start(f32[2,1024,256]{1,2,0:T(8,128)} %get-tuple-element.77), channel_id=1, source_target_pairs={{0,1},{1,2},{2,3},{4,5},{5,6},{6,7},{8,9},{9,10},{10,11},{12,13},{... | collective-permute-start | bytes 6291464 | tf_op jit(solution)/shard_map/ppermute | solution.py:52
  248.7 12.1 %copy-start.4 = (f32[2,1024,256]{1,2,0:T(8,128)}, f32[2,1024,256]{1,2,0:T(8,128)S(1)}, u32[]{:S(2)}) copy-start(f32[2,1024,256]{1,2,0:T(8,128)S(1)} %fusion.34) | copy-start | bytes 6291460
  253.2 21.0 %collective-permute-start.19 = (f32[1024,256]{0,1:T(8,128)S(1)}, f32[1024,256]{0,1:T(8,128)}, u32[]{:S(2)}, u32[]{:S(2)}) collective-permute-start(f32[1024,256]{0,1:T(8,128)S(1)} %fusion.81), channel_id=1, source_target_pairs={{4,0},{8,4},{12,8},{5,1},{9,5},{13,9},{6,2},{10,6},{14,10},{7,3},{... | collective-permute-start | bytes 3145736 | tf_op jit(solution)/shard_map/ppermute | solution.py:12
  282.7 16.4 %collective-permute-start = (f32[1024,256]{0,1:T(8,128)}, f32[1024,256]{0,1:T(8,128)}, u32[]{:S(2)}, u32[]{:S(2)}) collective-permute-start(f32[1024,256]{0,1:T(8,128)} %fusion.161), channel_id=1, source_target_pairs={{4,0},{8,4},{12,8},{5,1},{9,5},{13,9},{6,2},{10,6},{14,10},{7,3},{... | collective-permute-start | bytes 3145736 | tf_op jit(solution)/shard_map/while/body/eval_jaxpr/ppermute | solution.py:12
  307.5 16.4 %collective-permute-start = (f32[1024,256]{0,1:T(8,128)}, f32[1024,256]{0,1:T(8,128)}, u32[]{:S(2)}, u32[]{:S(2)}) collective-permute-start(f32[1024,256]{0,1:T(8,128)} %fusion.161), channel_id=1, source_target_pairs={{4,0},{8,4},{12,8},{5,1},{9,5},{13,9},{6,2},{10,6},{14,10},{7,3},{... | collective-permute-start | bytes 3145736 | tf_op jit(solution)/shard_map/while/body/eval_jaxpr/ppermute | solution.py:12
  (18 other events, 30.0 us)
